TPU v7x, 768 devices: a whole 4x8x12 slice. The times are simulated.
768 devices in a mesh: dp: 24 (over y, z_lo), seq: 32 (over x, z_hi, core).
Axes of the slice: x: 4, y: 8, z: 12 (z_hi: 4, z_lo: 3; z = z_hi * 3 + z_lo), core: 2. Of those that a mesh axis runs over, the one named last changes fastest.
Arguments:
- query: float32 [24, 256, 4096], P('dp', None, 'seq'), may hold values from -6 to 6
- key_in: float32 [24, 256, 4096], P('dp', None, 'seq'), may hold values from -6 to 6
- value: float32 [24, 256, 4096], P('dp', None, 'seq'), may hold values from -6 to 6
- grad_out: float32 [24, 256, 4096], P('dp', None, 'seq'), may hold values from -6 to 6
- filt: float32 [256, 4096], P('seq'), may hold values from -0.09375 to 0.09375
Outputs:
- output: float32 [24, 256, 4096], P('dp', None, 'seq')
- grad_query: float32 [24, 256, 4096], P('dp', None, 'seq')
- grad_key: float32 [24, 256, 4096], P('dp', None, 'seq')
- grad_value: float32 [24, 256, 4096], P('dp', None, 'seq')
- grad_filt: float32 [256, 4096], P('seq')
All inputs are finite; a program needn't handle non-finite values.
Results may differ from a plain program's by a relative error of at most 0.00016.
Values sent between devices are 32-bit elements; how exact they have to be, the bound alone decides.
No kernel may reach another device: no remote copies, remote signals or barrier semaphores. Data moves between devices by JAX's collectives and lax.ppermute only.
A program may use at most 32 MiB of HBM per device.

v0:
```python
import functools
import math

import jax
import jax.numpy as jnp
from jax import lax
from jax.sharding import PartitionSpec as P

highest = lax.Precision.HIGHEST


def dft_tables(rows, cols, total, sign):
    first = jnp.arange(rows, dtype=jnp.int32)
    second = jnp.arange(cols, dtype=jnp.int32)
    product = first[:, None] * second[None, :] % total
    angles = product.astype(jnp.float32) * (sign * 2.0 * math.pi / total)
    return (jnp.cos(angles), jnp.sin(angles))


def direct_last(real, imag, sign):
    length = real.shape[-1]
    cosine, sine = dft_tables(length, length, length, sign)
    out_real = jnp.einsum("...n,kn->...k", real, cosine, precision=highest) - jnp.einsum(
        "...n,kn->...k", imag, sine, precision=highest
    )
    out_imag = jnp.einsum("...n,kn->...k", imag, cosine, precision=highest) + jnp.einsum(
        "...n,kn->...k", real, sine, precision=highest
    )
    return (out_real, out_imag)


def transform(real, imag, sign):
    length = real.shape[-1]
    rest = 128
    radix = length // rest
    leading = real.shape[:-1]
    real = real.reshape(leading + (radix, rest))
    imag = imag.reshape(leading + (radix, rest))
    cosine, sine = dft_tables(radix, radix, radix, sign)
    part_real = jnp.einsum("kn,...nm->...km", cosine, real, precision=highest) - jnp.einsum(
        "kn,...nm->...km", sine, imag, precision=highest
    )
    part_imag = jnp.einsum("kn,...nm->...km", cosine, imag, precision=highest) + jnp.einsum(
        "kn,...nm->...km", sine, real, precision=highest
    )
    twiddle_cos, twiddle_sin = dft_tables(radix, rest, length, sign)
    turned_real = part_real * twiddle_cos - part_imag * twiddle_sin
    turned_imag = part_real * twiddle_sin + part_imag * twiddle_cos
    inner_real, inner_imag = direct_last(turned_real, turned_imag, sign)
    inner_real = jnp.swapaxes(inner_real, -1, -2).reshape(leading + (length,))
    inner_imag = jnp.swapaxes(inner_imag, -1, -2).reshape(leading + (length,))
    return (inner_real, inner_imag)


def convolve_all(gated, grad_conv, filt):
    length = gated.shape[-1]
    padded = 2 * length
    stacked = jnp.stack([gated[0], filt, grad_conv[0]])
    stacked = jnp.concatenate([stacked, jnp.zeros_like(stacked)], axis=-1)
    spec_real, spec_imag = transform(stacked, jnp.zeros_like(stacked), -1.0)
    g_re, f_re, d_re = (spec_real[0], spec_real[1], spec_real[2])
    g_im, f_im, d_im = (spec_imag[0], spec_imag[1], spec_imag[2])
    prod_real = jnp.stack(
        [f_re * g_re - f_im * g_im, f_re * d_re + f_im * d_im, g_re * d_re + g_im * d_im]
    )
    prod_imag = jnp.stack(
        [f_re * g_im + f_im * g_re, f_re * d_im - f_im * d_re, g_re * d_im - g_im * d_re]
    )
    back_real, back_imag = transform(prod_real, prod_imag, 1.0)
    result = back_real[:, :, :length] / padded
    return (result[0][None], result[1][None], result[2])


def sum_in_order(part, axis):
    size = lax.axis_size(axis)
    me = lax.axis_index(axis)
    held = {0: part}
    for shift in range(1, size):
        held[shift] = lax.ppermute(part, axis, [(j, (j + shift) % size) for j in range(size)])
    total = None
    for member in range(size):
        value = held[0]
        for shift in range(1, size):
            value = jnp.where((me - shift) % size == member, held[shift], value)
        total = value if total is None else total + value
    return total


def sum_by_doubling(part, axis):
    size = lax.axis_size(axis)
    step = 1
    while step < size:
        part = part + lax.ppermute(part, axis, [(j, j ^ step) for j in range(size)])
        step *= 2
    return part


def reduce_filter(part, dp_axes):
    if len(dp_axes) == 1:
        return lax.psum(part, dp_axes)
    wide, narrow = dp_axes
    return sum_by_doubling(sum_in_order(part, narrow), wide)


def body(query, key_in, value, grad_out, filt, dp_axes=("dp",)):
    batches = 1
    for axis in dp_axes:
        batches *= lax.axis_size(axis)
    parts = lax.axis_size("seq")
    length = filt.shape[1]
    channels = query.shape[1]
    local = query.shape[2]
    per = channels // parts
    gated = key_in[0] * value[0]
    grad_conv = grad_out[0] * query[0]
    sent = jnp.stack([gated, grad_conv]).reshape(2, parts, per, local)
    got = lax.all_to_all(sent, "seq", split_axis=1, concat_axis=1, tiled=True)
    got = jnp.swapaxes(got, 1, 2).reshape(2, per, length)
    conv, grad_gated, filt_local = convolve_all(got[0][None], got[1][None], filt)
    back = jnp.stack([conv[0], grad_gated[0]]).reshape(2, per, parts, local)
    back = jnp.swapaxes(back, 1, 2)
    back = lax.all_to_all(back, "seq", split_axis=1, concat_axis=1, tiled=True)
    back = back.reshape(2, 1, channels, local)
    conv_here, gated_grad_here = back[0], back[1]
    output = query * conv_here
    grad_query = grad_out * conv_here
    grad_key = gated_grad_here * value
    grad_value = gated_grad_here * key_in
    grad_filt = reduce_filter(filt_local, dp_axes) / math.sqrt(batches * length)
    return (output, grad_query, grad_key, grad_value, grad_filt)


def solution(mesh):
    from jax.sharding import Mesh

    batches = mesh.shape["dp"]
    narrow = 3
    wide = batches // narrow
    if batches % narrow == 0 and wide & (wide - 1) == 0:
        devices = mesh.devices.reshape(wide, narrow, mesh.shape["seq"])
        mesh = Mesh(devices, ("dp_wide", "dp_narrow", "seq"))
        dp_axes = ("dp_wide", "dp_narrow")
    else:
        dp_axes = ("dp",)
    fields = P(dp_axes, None, "seq")
    return jax.shard_map(
        functools.partial(body, dp_axes=dp_axes),
        mesh=mesh,
        in_specs=(fields, fields, fields, fields, P("seq", None)),
        out_specs=(fields, fields, fields, fields, P("seq", None)),
        check_vma=False,
    )
```

profile of v0, /device:TPU:128, one launch (start us, length us, event | category | flops | bytes accessed | tf_op | source)
XLA Modules:
  0.0 113.5 jit_solution(15486735971752486001)
XLA Ops:
  0.6 1.2 %multiply_bitcast_fusion = (f32[1,32,8,128]{3,2,0,1:T(8,128)S(1)}, f32[1,32,8,128]{3,2,0,1:T(8,128)S(1)}) fusion(f32[1,256,128]{2,1,0:T(8,128)} %param.8, f32[1,256,128]{2,1,0:T(8,128)} %param.5, f32[1,256,128]{2,1,0:T(8,128)} %param.6, f32[1,256,128]{2,1,0:T(8,128)} %param.7), kind=kLoop, calls=%fused_computation.58 | loop fusion | flops 65536 | bytes 786432 | tf_op jit(solution)/shard_map/stack | solution.py:116
  2.5 15.0 %all-to-all-start = ((f32[2,32,8,128]{3,2,0,1:T(8,128)}), f32[2,32,8,128]{3,2,0,1:T(8,128)S(1)}, u32[]{:S(2)}, u32[]{:S(2)}) async-start(f32[2,32,8,128]{3,2,0,1:T(8,128)} %pad_maximum_fusion), calls=%async_computation | async-start | bytes 524288 | tf_op jit(solution)/shard_map/all_to_all | solution.py:117
  18.4 17.3 %all-to-all-done = f32[2,32,8,128]{3,2,0,1:T(8,128)S(1)} async-done(((f32[2,32,8,128]{3,2,0,1:T(8,128)}), f32[2,32,8,128]{3,2,0,1:T(8,128)S(1)}, u32[]{:S(2)}, u32[]{:S(2)}) %all-to-all-start) | async-done | bytes 262176 | tf_op jit(solution)/shard_map/all_to_all | solution.py:117
  35.8 1.0 fusion.8
  37.4 1.0 fusion.5
  38.4 1.0 fusion.28
  39.4 1.0 fusion.27
  40.5 1.0 fusion.3
  41.5 1.0 fusion.4
  47.0 1.1 %fusion.2 = f32[3,8,64,128]{3,2,1,0:T(8,128)S(1)} fusion(f32[3,8,128,64]{2,3,1,0:T(8,128)S(1)} %fusion.56, f32[3,8,64,128]{3,2,1,0:T(8,128)S(1)} %constant_dynamic-update-slice_fusion.3), kind=kOutput, calls=%fused_computation.5 | convolution fusion | flops 151248896 | bytes 2359296 | tf_op jit(solution)/shard_map/kn,...nm->...km/dot_general | solution.py:40
  48.1 0.9 fusion.1
  49.1 1.0 fusion.14
  50.1 1.0 fusion
  52.2 2.1 %collective-permute-start.1 = (f32[8,4096]{1,0:T(8,128)S(1)}, f32[8,4096]{1,0:T(8,128)S(1)}, u32[]{:S(2)}, u32[]{:S(2)}) collective-permute-start(f32[8,4096]{1,0:T(8,128)S(1)} %slice_bitcast_fusion.1), channel_id=1, source_target_pairs={{0,32},{32,64},{64,0},{1,33},{33,65},{65,1},{2,34},{34,66},{66,2},... | collective-permute-start | bytes 393224 | tf_op jit(solution)/shard_map/ppermute | solution.py:79
  54.3 3.9 %collective-permute-start = (f32[8,4096]{1,0:T(8,128)S(1)}, f32[8,4096]{1,0:T(8,128)S(1)}, u32[]{:S(2)}, u32[]{:S(2)}) collective-permute-start(f32[8,4096]{1,0:T(8,128)S(1)} %slice_bitcast_fusion.1), channel_id=1, source_target_pairs={{0,64},{32,0},{64,32},{1,65},{33,1},{65,33},{2,66},{34,2},{66,34},... | collective-permute-start | bytes 393224 | tf_op jit(solution)/shard_map/ppermute | solution.py:79
  58.3 2.2 %collective-permute-done.1 = f32[8,4096]{1,0:T(8,128)S(1)} collective-permute-done((f32[8,4096]{1,0:T(8,128)S(1)}, f32[8,4096]{1,0:T(8,128)S(1)}, u32[]{:S(2)}, u32[]{:S(2)}) %collective-permute-start.1) | collective-permute-done | bytes 131104 | tf_op jit(solution)/shard_map/ppermute | solution.py:79
  60.4 3.2 %collective-permute-done = f32[8,4096]{1,0:T(8,128)S(1)} collective-permute-done((f32[8,4096]{1,0:T(8,128)S(1)}, f32[8,4096]{1,0:T(8,128)S(1)}, u32[]{:S(2)}, u32[]{:S(2)}) %collective-permute-start) | collective-permute-done | bytes 131104 | tf_op jit(solution)/shard_map/ppermute | solution.py:79
  63.7 3.5 %collective-permute-start.2 = (f32[8,4096]{1,0:T(8,128)S(1)}, f32[8,4096]{1,0:T(8,128)S(1)}, u32[]{:S(2)}, u32[]{:S(2)}) collective-permute-start(f32[8,4096]{1,0:T(8,128)S(1)} %select_add_fusion), channel_id=1, source_target_pairs={{0,96},{96,0},{192,288},{288,192},{384,480},{480,384},{576,672},{6... | collective-permute-start | bytes 393224 | tf_op jit(solution)/shard_map/ppermute | solution.py:93
  67.2 3.5 %collective-permute-done.2 = f32[8,4096]{1,0:T(8,128)S(1)} collective-permute-done((f32[8,4096]{1,0:T(8,128)S(1)}, f32[8,4096]{1,0:T(8,128)S(1)}, u32[]{:S(2)}, u32[]{:S(2)}) %collective-permute-start.2) | collective-permute-done | bytes 131104 | tf_op jit(solution)/shard_map/ppermute | solution.py:93
  70.7 4.5 %collective-permute-start.3 = (f32[8,4096]{1,0:T(8,128)S(1)}, f32[8,4096]{1,0:T(8,128)S(1)}, u32[]{:S(2)}, u32[]{:S(2)}) collective-permute-start(f32[8,4096]{1,0:T(8,128)S(1)} %add.193), channel_id=1, source_target_pairs={{0,192},{96,288},{192,0},{288,96},{384,576},{480,672},{576,384},{6... | collective-permute-start | bytes 393224 | tf_op jit(solution)/shard_map/ppermute | solution.py:93
  75.2 5.4 %collective-permute-done.3 = f32[8,4096]{1,0:T(8,128)S(1)} collective-permute-done((f32[8,4096]{1,0:T(8,128)S(1)}, f32[8,4096]{1,0:T(8,128)S(1)}, u32[]{:S(2)}, u32[]{:S(2)}) %collective-permute-start.3) | collective-permute-done | bytes 131104 | tf_op jit(solution)/shard_map/ppermute | solution.py:93
  80.6 7.7 %collective-permute-start.4 = (f32[8,4096]{1,0:T(8,128)S(1)}, f32[8,4096]{1,0:T(8,128)S(1)}, u32[]{:S(2)}, u32[]{:S(2)}) collective-permute-start(f32[8,4096]{1,0:T(8,128)S(1)} %add.194), channel_id=1, source_target_pairs={{0,384},{96,480},{192,576},{288,672},{384,0},{480,96},{576,192},{6... | collective-permute-start | bytes 393224 | tf_op jit(solution)/shard_map/ppermute | solution.py:93
  89.1 4.6 %all-to-all-start.1 = ((f32[2,32,8,128]{3,2,0,1:T(8,128)}), f32[2,32,8,128]{3,2,0,1:T(8,128)S(1)}, u32[]{:S(2)}, u32[]{:S(2)}) async-start(f32[2,32,8,128]{3,2,0,1:T(8,128)} %copy_bitcast_fusion), calls=%async_computation.1 | async-start | bytes 524288 | tf_op jit(solution)/shard_map/all_to_all | solution.py:122
  94.9 17.7 %all-to-all-done.1 = f32[2,32,8,128]{3,2,0,1:T(8,128)S(1)} async-done(((f32[2,32,8,128]{3,2,0,1:T(8,128)}), f32[2,32,8,128]{3,2,0,1:T(8,128)S(1)}, u32[]{:S(2)}, u32[]{:S(2)}) %all-to-all-start.1) | async-done | bytes 262176 | tf_op jit(solution)/shard_map/all_to_all | solution.py:122
  (50 shorter events, 10.4 us)
Async XLA Ops:
  0.6 35.1 %copy-start.4 = (f32[8,4096]{1,0:T(8,128)S(1)}, f32[8,4096]{1,0:T(8,128)}, u32[]{:S(2)}) copy-start(f32[8,4096]{1,0:T(8,128)} %param.9) | copy-start | bytes 393220
  2.5 33.2 %all-to-all-start = ((f32[2,32,8,128]{3,2,0,1:T(8,128)}), f32[2,32,8,128]{3,2,0,1:T(8,128)S(1)}, u32[]{:S(2)}, u32[]{:S(2)}) async-start(f32[2,32,8,128]{3,2,0,1:T(8,128)} %pad_maximum_fusion), calls=%async_computation | async-start | bytes 524288 | tf_op jit(solution)/shard_map/all_to_all | solution.py:117
  52.2 60.5 %copy-start = (f32[1,256,128]{2,1,0:T(8,128)S(1)}, f32[1,256,128]{2,1,0:T(8,128)}, u32[]{:S(2)}) copy-start(f32[1,256,128]{2,1,0:T(8,128)} %param.6) | copy-start | bytes 393220
  52.2 60.5 %copy-start.1 = (f32[1,256,128]{2,1,0:T(8,128)S(1)}, f32[1,256,128]{2,1,0:T(8,128)}, u32[]{:S(2)}) copy-start(f32[1,256,128]{2,1,0:T(8,128)} %param.8) | copy-start | bytes 393220
  52.2 60.5 %copy-start.2 = (f32[1,256,128]{2,1,0:T(8,128)S(1)}, f32[1,256,128]{2,1,0:T(8,128)}, u32[]{:S(2)}) copy-start(f32[1,256,128]{2,1,0:T(8,128)} %param.5) | copy-start | bytes 393220
  52.2 60.5 %copy-start.3 = (f32[1,256,128]{2,1,0:T(8,128)S(1)}, f32[1,256,128]{2,1,0:T(8,128)}, u32[]{:S(2)}) copy-start(f32[1,256,128]{2,1,0:T(8,128)} %param.7) | copy-start | bytes 393220
  52.2 8.2 %collective-permute-start.1 = (f32[8,4096]{1,0:T(8,128)S(1)}, f32[8,4096]{1,0:T(8,128)S(1)}, u32[]{:S(2)}, u32[]{:S(2)}) collective-permute-start(f32[8,4096]{1,0:T(8,128)S(1)} %slice_bitcast_fusion.1), channel_id=1, source_target_pairs={{0,32},{32,64},{64,0},{1,33},{33,65},{65,1},{2,34},{34,66},{66,2},... | collective-permute-start | bytes 393224 | tf_op jit(solution)/shard_map/ppermute | solution.py:79
  54.3 9.3 %collective-permute-start = (f32[8,4096]{1,0:T(8,128)S(1)}, f32[8,4096]{1,0:T(8,128)S(1)}, u32[]{:S(2)}, u32[]{:S(2)}) collective-permute-start(f32[8,4096]{1,0:T(8,128)S(1)} %slice_bitcast_fusion.1), channel_id=1, source_target_pairs={{0,64},{32,0},{64,32},{1,65},{33,1},{65,33},{2,66},{34,2},{66,34},... | collective-permute-start | bytes 393224 | tf_op jit(solution)/shard_map/ppermute | solution.py:79
  63.7 7.0 %collective-permute-start.2 = (f32[8,4096]{1,0:T(8,128)S(1)}, f32[8,4096]{1,0:T(8,128)S(1)}, u32[]{:S(2)}, u32[]{:S(2)}) collective-permute-start(f32[8,4096]{1,0:T(8,128)S(1)} %select_add_fusion), channel_id=1, source_target_pairs={{0,96},{96,0},{192,288},{288,192},{384,480},{480,384},{576,672},{6... | collective-permute-start | bytes 393224 | tf_op jit(solution)/shard_map/ppermute | solution.py:93
  70.7 9.9 %collective-permute-start.3 = (f32[8,4096]{1,0:T(8,128)S(1)}, f32[8,4096]{1,0:T(8,128)S(1)}, u32[]{:S(2)}, u32[]{:S(2)}) collective-permute-start(f32[8,4096]{1,0:T(8,128)S(1)} %add.193), channel_id=1, source_target_pairs={{0,192},{96,288},{192,0},{288,96},{384,576},{480,672},{576,384},{6... | collective-permute-start | bytes 393224 | tf_op jit(solution)/shard_map/ppermute | solution.py:93
  80.6 13.6 %collective-permute-start.4 = (f32[8,4096]{1,0:T(8,128)S(1)}, f32[8,4096]{1,0:T(8,128)S(1)}, u32[]{:S(2)}, u32[]{:S(2)}) collective-permute-start(f32[8,4096]{1,0:T(8,128)S(1)} %add.194), channel_id=1, source_target_pairs={{0,384},{96,480},{192,576},{288,672},{384,0},{480,96},{576,192},{6... | collective-permute-start | bytes 393224 | tf_op jit(solution)/shard_map/ppermute | solution.py:93
  89.1 23.6 %all-to-all-start.1 = ((f32[2,32,8,128]{3,2,0,1:T(8,128)}), f32[2,32,8,128]{3,2,0,1:T(8,128)S(1)}, u32[]{:S(2)}, u32[]{:S(2)}) async-start(f32[2,32,8,128]{3,2,0,1:T(8,128)} %copy_bitcast_fusion), calls=%async_computation.1 | async-start | bytes 524288 | tf_op jit(solution)/shard_map/all_to_all | solution.py:122
where the time goes:
time: 114 us; the launch traced here: 113 us
  waiting for transfers between devices  49.8 us (44%)
  starting transfers between devices  41.3 us (36%)
  matrix products  13.3 us (12%)
  other arithmetic  4.07 us (4%)
  local copies, waits for them, and re-layouts  3.88 us (3%)
    all_to_all x1, waiting for transfers between devices, body(): back = lax.all_to_all(back, 'seq', split_axis=1, concat_axis=1, tiled=True)  17.7 us
    all_to_all x1, waiting for transfers between devices, body(): got = lax.all_to_all(sent, 'seq', split_axis=1, concat_axis=1, tiled=True)  17.3 us
    ppermute x3, starting transfers between devices, sum_by_doubling(): part = part + lax.ppermute(part, axis, [(j, j ^ step) for j in range(size)])  15.7 us
    all_to_all x1, starting transfers between devices, body(): got = lax.all_to_all(sent, 'seq', split_axis=1, concat_axis=1, tiled=True)  15 us
    ppermute x3, waiting for transfers between devices, sum_by_doubling(): part = part + lax.ppermute(part, axis, [(j, j ^ step) for j in range(size)])  9.48 us
    ppermute x2, starting transfers between devices, sum_in_order(): lax.ppermute(part, axis, [(j, (j + shift) % size) for j in range(size)])  5.97 us
    ppermute x2, waiting for transfers between devices, sum_in_order(): lax.ppermute(part, axis, [(j, (j + shift) % size) for j in range(size)])  5.35 us
    all_to_all x1, starting transfers between devices, body(): back = lax.all_to_all(back, 'seq', split_axis=1, concat_axis=1, tiled=True)  4.63 us
  transfers between devices with their start and end apart: 7, of which 7 were waited for; matrix products, arithmetic and copies ran while one was open for 2% of the time, Pallas kernels for 0%

commit v1 on v0

--- a/solution.py
+++ b/solution.py
@@ -17,58 +17,63 @@
     return (jnp.cos(angles), jnp.sin(angles))
 
 
-def direct_last(real, imag, sign):
-    length = real.shape[-1]
-    cosine, sine = dft_tables(length, length, length, sign)
-    out_real = jnp.einsum("...n,kn->...k", real, cosine, precision=highest) - jnp.einsum(
-        "...n,kn->...k", imag, sine, precision=highest
-    )
-    out_imag = jnp.einsum("...n,kn->...k", imag, cosine, precision=highest) + jnp.einsum(
-        "...n,kn->...k", real, sine, precision=highest
-    )
-    return (out_real, out_imag)
+def mix_table(size, sign):
+    cosine, sine = dft_tables(size, size, size, sign)
+    top = jnp.concatenate([cosine.T, sine.T], axis=1)
+    bottom = jnp.concatenate([-sine.T, cosine.T], axis=1)
+    return jnp.concatenate([top, bottom], axis=0)
 
 
-def transform(real, imag, sign):
-    length = real.shape[-1]
-    rest = 128
-    radix = length // rest
-    leading = real.shape[:-1]
-    real = real.reshape(leading + (radix, rest))
-    imag = imag.reshape(leading + (radix, rest))
-    cosine, sine = dft_tables(radix, radix, radix, sign)
-    part_real = jnp.einsum("kn,...nm->...km", cosine, real, precision=highest) - jnp.einsum(
-        "kn,...nm->...km", sine, imag, precision=highest
+def forward(signal, major, minor):
+    padded = major * minor
+    lead = signal.shape[:-1]
+    held = signal.shape[-1] // minor
+    blocks = signal.reshape(lead + (held, minor))
+    cosine, sine = dft_tables(major, held, major, -1.0)
+    part = jnp.einsum("kn,...nm->...km", jnp.concatenate([cosine, sine], axis=0), blocks, precision=highest)
+    part_real, part_imag = part[..., :major, :], part[..., major:, :]
+    twiddle_cos, twiddle_sin = dft_tables(major, minor, padded, -1.0)
+    turned = jnp.concatenate(
+        [part_real * twiddle_cos - part_imag * twiddle_sin, part_real * twiddle_sin + part_imag * twiddle_cos],
+        axis=-1,
     )
-    part_imag = jnp.einsum("kn,...nm->...km", cosine, imag, precision=highest) + jnp.einsum(
-        "kn,...nm->...km", sine, real, precision=highest
+    return jnp.einsum("...n,nk->...k", turned, mix_table(minor, -1.0), precision=highest)
+
+
+def inverse_real(spectrum, major, minor, keep):
+    padded = major * minor
+    mixed = jnp.einsum("...n,nk->...k", spectrum, mix_table(minor, 1.0), precision=highest)
+    mixed_real, mixed_imag = mixed[..., :minor], mixed[..., minor:]
+    twiddle_cos, twiddle_sin = dft_tables(major, minor, padded, 1.0)
+    turned = jnp.concatenate(
+        [mixed_real * twiddle_cos - mixed_imag * twiddle_sin, mixed_real * twiddle_sin + mixed_imag * twiddle_cos],
+        axis=-2,
     )
-    twiddle_cos, twiddle_sin = dft_tables(radix, rest, length, sign)
-    turned_real = part_real * twiddle_cos - part_imag * twiddle_sin
-    turned_imag = part_real * twiddle_sin + part_imag * twiddle_cos
-    inner_real, inner_imag = direct_last(turned_real, turned_imag, sign)
-    inner_real = jnp.swapaxes(inner_real, -1, -2).reshape(leading + (length,))
-    inner_imag = jnp.swapaxes(inner_imag, -1, -2).reshape(leading + (length,))
-    return (inner_real, inner_imag)
+    rows = keep // minor
+    cosine, sine = dft_tables(rows, major, major, 1.0)
+    out = jnp.einsum("kn,...nm->...km", jnp.concatenate([cosine, -sine], axis=1), turned, precision=highest)
+    return out.reshape(out.shape[:-2] + (rows * minor,))
+
+
+def times(a, b, minor, conjugate_a):
+    a_re, a_im = a[..., :minor], a[..., minor:]
+    b_re, b_im = b[..., :minor], b[..., minor:]
+    if conjugate_a:
+        return jnp.concatenate([a_re * b_re + a_im * b_im, a_re * b_im - a_im * b_re], axis=-1)
+    return jnp.concatenate([a_re * b_re - a_im * b_im, a_re * b_im + a_im * b_re], axis=-1)
 
 
 def convolve_all(gated, grad_conv, filt):
     length = gated.shape[-1]
     padded = 2 * length
-    stacked = jnp.stack([gated[0], filt, grad_conv[0]])
-    stacked = jnp.concatenate([stacked, jnp.zeros_like(stacked)], axis=-1)
-    spec_real, spec_imag = transform(stacked, jnp.zeros_like(stacked), -1.0)
-    g_re, f_re, d_re = (spec_real[0], spec_real[1], spec_real[2])
-    g_im, f_im, d_im = (spec_imag[0], spec_imag[1], spec_imag[2])
-    prod_real = jnp.stack(
-        [f_re * g_re - f_im * g_im, f_re * d_re + f_im * d_im, g_re * d_re + g_im * d_im]
-    )
-    prod_imag = jnp.stack(
-        [f_re * g_im + f_im * g_re, f_re * d_im - f_im * d_re, g_re * d_im - g_im * d_re]
-    )
-    back_real, back_imag = transform(prod_real, prod_imag, 1.0)
-    result = back_real[:, :, :length] / padded
-    return (result[0][None], result[1][None], result[2])
+    minor = 128
+    major = padded // minor
+    spec = forward(jnp.stack([gated, filt, grad_conv]), major, minor)
+    g_spec, f_spec, d_spec = spec[0], spec[1], spec[2]
+    pair = jnp.stack([times(f_spec, g_spec, minor, False), times(f_spec, d_spec, minor, True)])
+    both = inverse_real(pair, major, minor, length) / padded
+    filt_local = inverse_real(times(g_spec, d_spec, minor, True), major, minor, length) / padded
+    return (both[0], both[1], filt_local)
 
 
 def sum_in_order(part, axis):
@@ -116,8 +121,8 @@
     sent = jnp.stack([gated, grad_conv]).reshape(2, parts, per, local)
     got = lax.all_to_all(sent, "seq", split_axis=1, concat_axis=1, tiled=True)
     got = jnp.swapaxes(got, 1, 2).reshape(2, per, length)
-    conv, grad_gated, filt_local = convolve_all(got[0][None], got[1][None], filt)
-    back = jnp.stack([conv[0], grad_gated[0]]).reshape(2, per, parts, local)
+    conv, grad_gated, filt_local = convolve_all(got[0], got[1], filt)
+    back = jnp.stack([conv, grad_gated]).reshape(2, per, parts, local)
     back = jnp.swapaxes(back, 1, 2)
     back = lax.all_to_all(back, "seq", split_axis=1, concat_axis=1, tiled=True)
     back = back.reshape(2, 1, channels, local)

time: 114 us -> 104 us (0.912)
  matrix products: 13.3 us -> 5.58 us
  local copies, waits for them, and re-layouts: 3.88 us -> 1.99 us
  waiting for transfers between devices: 49.8 us -> 48 us
    dot_general x14 -> x6, matrix products: 13.3 us -> 5.58 us  [the longest x2 1.56 us: inverse_real(): jnp.einsum('...n,nk->...k', spectrum, mix_table(minor, 1.0), precision=hi...]
    sub x7 -> x0, local copies, waits for them, and re-layouts: 1.48 us -> none  [the longest x1 0.47 us: direct_last(): jnp.einsum('...n,kn->...k', real, cosine, precision=highest)]
  transfers between devices with their start and end apart: 7 -> 7, of which waited for: 7 -> 7; matrix products, arithmetic and copies ran while one was open for 2% -> 5% of each run, Pallas kernels for 0% -> 0%
where the time goes in v1:
time: 104 us; the launch traced here: 103 us
  waiting for transfers between devices  48 us (46%)
  starting transfers between devices  41.3 us (40%)
  matrix products  5.58 us (5%)
  other arithmetic  5.14 us (5%)
  local copies, waits for them, and re-layouts  1.99 us (2%)
    all_to_all x1, waiting for transfers between devices, body(): back = lax.all_to_all(back, 'seq', split_axis=1, concat_axis=1, tiled=True)  17.5 us
    all_to_all x1, waiting for transfers between devices, body(): got = lax.all_to_all(sent, 'seq', split_axis=1, concat_axis=1, tiled=True)  16.5 us
    ppermute x3, starting transfers between devices, sum_by_doubling(): part = part + lax.ppermute(part, axis, [(j, j ^ step) for j in range(size)])  15.7 us
    all_to_all x1, starting transfers between devices, body(): got = lax.all_to_all(sent, 'seq', split_axis=1, concat_axis=1, tiled=True)  15 us
    ppermute x3, waiting for transfers between devices, sum_by_doubling(): part = part + lax.ppermute(part, axis, [(j, j ^ step) for j in range(size)])  9.02 us
    ppermute x2, starting transfers between devices, sum_in_order(): lax.ppermute(part, axis, [(j, (j + shift) % size) for j in range(size)])  6.74 us
    ppermute x2, waiting for transfers between devices, sum_in_order(): lax.ppermute(part, axis, [(j, (j + shift) % size) for j in range(size)])  4.95 us
    all_to_all x1, starting transfers between devices, body(): back = lax.all_to_all(back, 'seq', split_axis=1, concat_axis=1, tiled=True)  3.87 us
  transfers between devices with their start and end apart: 7, of which 7 were waited for; matrix products, arithmetic and copies ran while one was open for 5% of the time, Pallas kernels for 0%

profile of v1, /device:TPU:128, one launch (start us, length us, event | category | flops | bytes accessed | tf_op | source)
XLA Modules:
  0.0 103.0 jit_solution(11925028435072171761)
XLA Ops:
  0.6 1.2 %multiply_bitcast_fusion = (f32[1,32,8,128]{3,2,1,0:T(8,128)S(1)}, f32[1,32,8,128]{3,2,1,0:T(8,128)S(1)}) fusion(f32[1,256,128]{2,1,0:T(8,128)} %param.8, f32[1,256,128]{2,1,0:T(8,128)} %param.5, f32[1,256,128]{2,1,0:T(8,128)} %param.6, f32[1,256,128]{2,1,0:T(8,128)} %param.7), kind=kLoop, calls=%fused_computation.63 | loop fusion | flops 65536 | bytes 786432 | tf_op jit(solution)/shard_map/stack | solution.py:121
  1.8 0.7 copy.14
  2.6 15.0 %all-to-all-start = ((f32[2,32,8,128]{3,2,0,1:T(8,128)}), f32[2,32,8,128]{3,2,0,1:T(8,128)S(1)}, u32[]{:S(2)}, u32[]{:S(2)}) async-start(f32[2,32,8,128]{3,2,0,1:T(8,128)} %copy.14), calls=%async_computation | async-start | bytes 524288 | tf_op jit(solution)/shard_map/all_to_all | solution.py:122
  19.2 16.5 %all-to-all-done = f32[2,32,8,128]{3,2,0,1:T(8,128)S(1)} async-done(((f32[2,32,8,128]{3,2,0,1:T(8,128)}), f32[2,32,8,128]{3,2,0,1:T(8,128)S(1)}, u32[]{:S(2)}, u32[]{:S(2)}) %all-to-all-start) | async-done | bytes 262176 | tf_op jit(solution)/shard_map/all_to_all | solution.py:122
  35.9 1.5 %convolution_bitcast_fusion = f32[3,8,128,128]{3,2,1,0:T(8,128)S(1)} fusion(f32[1,8,32,128]{3,2,1,0:T(8,128)S(1)} %get-tuple-element.27, f32[1,8,32,128]{3,2,1,0:T(8,128)S(1)} %copy.34, f32[1,8,32,128]{3,2,1,0:T(8,128)S(1)} %get-tuple-element.26, f32[64,32]{0,1:T(8,128)S(1)} %get-tuple-element.30, f32[64,32]{0,1:T(8,128)S(1)} %get-tuple-element.31), kind=kOutput, calls=%fused_computation.4 | convolution fusion | flops 151195648 | bytes 1982464 | tf_op jit(solution)/shard_map/kn,...nm->...km/dot_general | solution.py:33
  37.7 1.4 %fusion = f32[3,8,64,256]{3,2,1,0:T(8,128)S(1)} fusion(f32[3,8,64,128]{3,2,1,0:T(8,128)S(1)} %get-tuple-element.6, f32[3,8,64,128]{3,2,1,0:T(8,128)S(1)} %get-tuple-element.5, f32[128,128]{1,0:T(8,128)S(1)} %get-tuple-element.35, f32[128,128]{1,0:T(8,128)S(1)} %fusion.47, f32[128,128]{1,0:T(8,128)S(1)} %get-tuple-element.34), kind=kOutput, calls=%fused_computation | convolution fusion | flops 1208549376 | bytes 3342336 | tf_op jit(solution)/shard_map/...n,nk->...k/dot_general | solution.py:40
  39.4 0.6 fusion.13
  40.6 3.2 %collective-permute-start = (f32[8,4096]{1,0:T(8,128)S(1)}, f32[8,4096]{1,0:T(8,128)S(1)}, u32[]{:S(2)}, u32[]{:S(2)}) collective-permute-start(f32[8,4096]{1,0:T(8,128)S(1)} %bitcast.78), channel_id=1, source_target_pairs={{0,64},{32,0},{64,32},{1,65},{33,1},{65,33},{2,66},{34,2},{66,34},... | collective-permute-start | bytes 393224 | tf_op jit(solution)/shard_map/ppermute | solution.py:84
  43.8 3.6 %collective-permute-start.1 = (f32[8,4096]{1,0:T(8,128)S(1)}, f32[8,4096]{1,0:T(8,128)S(1)}, u32[]{:S(2)}, u32[]{:S(2)}) collective-permute-start(f32[8,4096]{1,0:T(8,128)S(1)} %bitcast.79), channel_id=1, source_target_pairs={{0,32},{32,64},{64,0},{1,33},{33,65},{65,1},{2,34},{34,66},{66,2},... | collective-permute-start | bytes 393224 | tf_op jit(solution)/shard_map/ppermute | solution.py:84
  47.4 2.3 %collective-permute-done = f32[8,4096]{1,0:T(8,128)S(1)} collective-permute-done((f32[8,4096]{1,0:T(8,128)S(1)}, f32[8,4096]{1,0:T(8,128)S(1)}, u32[]{:S(2)}, u32[]{:S(2)}) %collective-permute-start) | collective-permute-done | bytes 131104 | tf_op jit(solution)/shard_map/ppermute | solution.py:84
  49.8 2.6 %collective-permute-done.1 = f32[8,4096]{1,0:T(8,128)S(1)} collective-permute-done((f32[8,4096]{1,0:T(8,128)S(1)}, f32[8,4096]{1,0:T(8,128)S(1)}, u32[]{:S(2)}, u32[]{:S(2)}) %collective-permute-start.1) | collective-permute-done | bytes 131104 | tf_op jit(solution)/shard_map/ppermute | solution.py:84
  52.5 3.5 %collective-permute-start.2 = (f32[8,4096]{1,0:T(8,128)S(1)}, f32[8,4096]{1,0:T(8,128)S(1)}, u32[]{:S(2)}, u32[]{:S(2)}) collective-permute-start(f32[8,4096]{1,0:T(8,128)S(1)} %select_add_fusion), channel_id=1, source_target_pairs={{0,96},{96,0},{192,288},{288,192},{384,480},{480,384},{576,672},{6... | collective-permute-start | bytes 393224 | tf_op jit(solution)/shard_map/ppermute | solution.py:98
  56.1 3.8 %collective-permute-done.2 = f32[8,4096]{1,0:T(8,128)S(1)} collective-permute-done((f32[8,4096]{1,0:T(8,128)S(1)}, f32[8,4096]{1,0:T(8,128)S(1)}, u32[]{:S(2)}, u32[]{:S(2)}) %collective-permute-start.2) | collective-permute-done | bytes 131104 | tf_op jit(solution)/shard_map/ppermute | solution.py:98
  59.8 4.5 %collective-permute-start.3 = (f32[8,4096]{1,0:T(8,128)S(1)}, f32[8,4096]{1,0:T(8,128)S(1)}, u32[]{:S(2)}, u32[]{:S(2)}) collective-permute-start(f32[8,4096]{1,0:T(8,128)S(1)} %add.158), channel_id=1, source_target_pairs={{0,192},{96,288},{192,0},{288,96},{384,576},{480,672},{576,384},{6... | collective-permute-start | bytes 393224 | tf_op jit(solution)/shard_map/ppermute | solution.py:98
  64.3 1.0 fusion.6
  65.3 4.7 %collective-permute-done.3 = f32[8,4096]{1,0:T(8,128)S(1)} collective-permute-done((f32[8,4096]{1,0:T(8,128)S(1)}, f32[8,4096]{1,0:T(8,128)S(1)}, u32[]{:S(2)}, u32[]{:S(2)}) %collective-permute-start.3) | collective-permute-done | bytes 131104 | tf_op jit(solution)/shard_map/ppermute | solution.py:98
  70.0 7.7 %collective-permute-start.4 = (f32[8,4096]{1,0:T(8,128)S(1)}, f32[8,4096]{1,0:T(8,128)S(1)}, u32[]{:S(2)}, u32[]{:S(2)}) collective-permute-start(f32[8,4096]{1,0:T(8,128)S(1)} %add.159), channel_id=1, source_target_pairs={{0,384},{96,480},{192,576},{288,672},{384,0},{480,96},{576,192},{6... | collective-permute-start | bytes 393224 | tf_op jit(solution)/shard_map/ppermute | solution.py:98
  78.0 0.7 fusion.4
  78.7 0.9 copy.16
  79.6 3.9 %all-to-all-start.1 = ((f32[2,32,8,128]{3,2,0,1:T(8,128)}), f32[2,32,8,128]{3,2,0,1:T(8,128)S(1)}, u32[]{:S(2)}, u32[]{:S(2)}) async-start(f32[2,32,8,128]{3,2,0,1:T(8,128)} %copy.16), calls=%async_computation.1 | async-start | bytes 524288 | tf_op jit(solution)/shard_map/all_to_all | solution.py:127
  83.4 0.6 collective-permute-done.4
  84.0 0.7 add_multiply_fusion
  84.7 17.5 %all-to-all-done.1 = f32[2,32,8,128]{3,2,0,1:T(8,128)S(1)} async-done(((f32[2,32,8,128]{3,2,0,1:T(8,128)}), f32[2,32,8,128]{3,2,0,1:T(8,128)S(1)}, u32[]{:S(2)}, u32[]{:S(2)}) %all-to-all-start.1) | async-done | bytes 262176 | tf_op jit(solution)/shard_map/all_to_all | solution.py:127
  102.2 0.8 fusion.35
  (35 shorter events, 3.3 us)
Async XLA Ops:
  0.6 17.1 %copy-start.4 = (f32[8,4096]{1,0:T(8,128)S(1)}, f32[8,4096]{1,0:T(8,128)}, u32[]{:S(2)}) copy-start(f32[8,4096]{1,0:T(8,128)} %param.9) | copy-start | bytes 393220
  2.6 33.2 %all-to-all-start = ((f32[2,32,8,128]{3,2,0,1:T(8,128)}), f32[2,32,8,128]{3,2,0,1:T(8,128)S(1)}, u32[]{:S(2)}, u32[]{:S(2)}) async-start(f32[2,32,8,128]{3,2,0,1:T(8,128)} %copy.14), calls=%async_computation | async-start | bytes 524288 | tf_op jit(solution)/shard_map/all_to_all | solution.py:122
  40.6 9.2 %collective-permute-start = (f32[8,4096]{1,0:T(8,128)S(1)}, f32[8,4096]{1,0:T(8,128)S(1)}, u32[]{:S(2)}, u32[]{:S(2)}) collective-permute-start(f32[8,4096]{1,0:T(8,128)S(1)} %bitcast.78), channel_id=1, source_target_pairs={{0,64},{32,0},{64,32},{1,65},{33,1},{65,33},{2,66},{34,2},{66,34},... | collective-permute-start | bytes 393224 | tf_op jit(solution)/shard_map/ppermute | solution.py:84
  43.8 8.6 %collective-permute-start.1 = (f32[8,4096]{1,0:T(8,128)S(1)}, f32[8,4096]{1,0:T(8,128)S(1)}, u32[]{:S(2)}, u32[]{:S(2)}) collective-permute-start(f32[8,4096]{1,0:T(8,128)S(1)} %bitcast.79), channel_id=1, source_target_pairs={{0,32},{32,64},{64,0},{1,33},{33,65},{65,1},{2,34},{34,66},{66,2},... | collective-permute-start | bytes 393224 | tf_op jit(solution)/shard_map/ppermute | solution.py:84
  52.5 7.3 %collective-permute-start.2 = (f32[8,4096]{1,0:T(8,128)S(1)}, f32[8,4096]{1,0:T(8,128)S(1)}, u32[]{:S(2)}, u32[]{:S(2)}) collective-permute-start(f32[8,4096]{1,0:T(8,128)S(1)} %select_add_fusion), channel_id=1, source_target_pairs={{0,96},{96,0},{192,288},{288,192},{384,480},{480,384},{576,672},{6... | collective-permute-start | bytes 393224 | tf_op jit(solution)/shard_map/ppermute | solution.py:98
  59.8 10.2 %collective-permute-start.3 = (f32[8,4096]{1,0:T(8,128)S(1)}, f32[8,4096]{1,0:T(8,128)S(1)}, u32[]{:S(2)}, u32[]{:S(2)}) collective-permute-start(f32[8,4096]{1,0:T(8,128)S(1)} %add.158), channel_id=1, source_target_pairs={{0,192},{96,288},{192,0},{288,96},{384,576},{480,672},{576,384},{6... | collective-permute-start | bytes 393224 | tf_op jit(solution)/shard_map/ppermute | solution.py:98
  70.0 14.0 %collective-permute-start.4 = (f32[8,4096]{1,0:T(8,128)S(1)}, f32[8,4096]{1,0:T(8,128)S(1)}, u32[]{:S(2)}, u32[]{:S(2)}) collective-permute-start(f32[8,4096]{1,0:T(8,128)S(1)} %add.159), channel_id=1, source_target_pairs={{0,384},{96,480},{192,576},{288,672},{384,0},{480,96},{576,192},{6... | collective-permute-start | bytes 393224 | tf_op jit(solution)/shard_map/ppermute | solution.py:98
  77.9 24.3 %copy-start = (f32[1,256,128]{2,1,0:T(8,128)S(1)}, f32[1,256,128]{2,1,0:T(8,128)}, u32[]{:S(2)}) copy-start(f32[1,256,128]{2,1,0:T(8,128)} %param.6) | copy-start | bytes 393220
  78.0 24.3 %copy-start.1 = (f32[1,256,128]{2,1,0:T(8,128)S(1)}, f32[1,256,128]{2,1,0:T(8,128)}, u32[]{:S(2)}) copy-start(f32[1,256,128]{2,1,0:T(8,128)} %param.8) | copy-start | bytes 393220
  78.0 24.3 %copy-start.2 = (f32[1,256,128]{2,1,0:T(8,128)S(1)}, f32[1,256,128]{2,1,0:T(8,128)}, u32[]{:S(2)}) copy-start(f32[1,256,128]{2,1,0:T(8,128)} %param.5) | copy-start | bytes 393220
  78.0 24.3 %copy-start.3 = (f32[1,256,128]{2,1,0:T(8,128)S(1)}, f32[1,256,128]{2,1,0:T(8,128)}, u32[]{:S(2)}) copy-start(f32[1,256,128]{2,1,0:T(8,128)} %param.7) | copy-start | bytes 393220
  79.6 22.6 %all-to-all-start.1 = ((f32[2,32,8,128]{3,2,0,1:T(8,128)}), f32[2,32,8,128]{3,2,0,1:T(8,128)S(1)}, u32[]{:S(2)}, u32[]{:S(2)}) async-start(f32[2,32,8,128]{3,2,0,1:T(8,128)} %copy.16), calls=%async_computation.1 | async-start | bytes 524288 | tf_op jit(solution)/shard_map/all_to_all | solution.py:127

commit v2 on v1

--- a/solution.py
+++ b/solution.py
@@ -5,6 +5,7 @@
 import jax.numpy as jnp
 from jax import lax
 from jax.sharding import PartitionSpec as P
+
 
 highest = lax.Precision.HIGHEST
 
@@ -104,10 +105,15 @@
     if len(dp_axes) == 1:
         return lax.psum(part, dp_axes)
     wide, narrow = dp_axes
-    return sum_by_doubling(sum_in_order(part, narrow), wide)
+    part = sum_in_order(part, narrow)
+    return sum_by_doubling(part, wide)
 
 
 def body(query, key_in, value, grad_out, filt, dp_axes=("dp",)):
+    return body_steps(query, key_in, value, grad_out, filt, dp_axes)
+
+
+def body_steps(query, key_in, value, grad_out, filt, dp_axes):
     batches = 1
     for axis in dp_axes:
         batches *= lax.axis_size(axis)

time: 104 us -> 104 us (level)
  no operation moved by 1% of the time
where the time goes in v2:
time: 104 us; the launch traced here: 103 us
  waiting for transfers between devices  48 us (46%)
  starting transfers between devices  41.3 us (40%)
  matrix products  5.58 us (5%)
  other arithmetic  5.14 us (5%)
  local copies, waits for them, and re-layouts  1.99 us (2%)
    all_to_all x1, waiting for transfers between devices, body_steps(): back = lax.all_to_all(back, 'seq', split_axis=1, concat_axis=1, tiled=True)  17.5 us
    all_to_all x1, waiting for transfers between devices, body_steps(): got = lax.all_to_all(sent, 'seq', split_axis=1, concat_axis=1, tiled=True)  16.5 us
    ppermute x3, starting transfers between devices, sum_by_doubling(): part = part + lax.ppermute(part, axis, [(j, j ^ step) for j in range(size)])  15.7 us
    all_to_all x1, starting transfers between devices, body_steps(): got = lax.all_to_all(sent, 'seq', split_axis=1, concat_axis=1, tiled=True)  15 us
    ppermute x3, waiting for transfers between devices, sum_by_doubling(): part = part + lax.ppermute(part, axis, [(j, j ^ step) for j in range(size)])  9.02 us
    ppermute x2, starting transfers between devices, sum_in_order(): lax.ppermute(part, axis, [(j, (j + shift) % size) for j in range(size)])  6.74 us
    ppermute x2, waiting for transfers between devices, sum_in_order(): lax.ppermute(part, axis, [(j, (j + shift) % size) for j in range(size)])  4.95 us
    all_to_all x1, starting transfers between devices, body_steps(): back = lax.all_to_all(back, 'seq', split_axis=1, concat_axis=1, tiled=True)  3.87 us
  transfers between devices with their start and end apart: 7, of which 7 were waited for; matrix products, arithmetic and copies ran while one was open for 5% of the time, Pallas kernels for 0%

profile of v2, /device:TPU:128, one launch (start us, length us, event | category | flops | bytes accessed | tf_op | source)
XLA Modules:
  0.0 103.0 jit_solution(11925028435072171761)
XLA Ops:
  0.6 1.2 %multiply_bitcast_fusion = (f32[1,32,8,128]{3,2,1,0:T(8,128)S(1)}, f32[1,32,8,128]{3,2,1,0:T(8,128)S(1)}) fusion(f32[1,256,128]{2,1,0:T(8,128)} %param.8, f32[1,256,128]{2,1,0:T(8,128)} %param.5, f32[1,256,128]{2,1,0:T(8,128)} %param.6, f32[1,256,128]{2,1,0:T(8,128)} %param.7), kind=kLoop, calls=%fused_computation.63 | loop fusion | flops 65536 | bytes 786432 | tf_op jit(solution)/shard_map/stack | solution.py:127
  1.8 0.7 copy.14
  2.6 15.0 %all-to-all-start = ((f32[2,32,8,128]{3,2,0,1:T(8,128)}), f32[2,32,8,128]{3,2,0,1:T(8,128)S(1)}, u32[]{:S(2)}, u32[]{:S(2)}) async-start(f32[2,32,8,128]{3,2,0,1:T(8,128)} %copy.14), calls=%async_computation | async-start | bytes 524288 | tf_op jit(solution)/shard_map/all_to_all | solution.py:128
  19.2 16.5 %all-to-all-done = f32[2,32,8,128]{3,2,0,1:T(8,128)S(1)} async-done(((f32[2,32,8,128]{3,2,0,1:T(8,128)}), f32[2,32,8,128]{3,2,0,1:T(8,128)S(1)}, u32[]{:S(2)}, u32[]{:S(2)}) %all-to-all-start) | async-done | bytes 262176 | tf_op jit(solution)/shard_map/all_to_all | solution.py:128
  35.9 1.5 %convolution_bitcast_fusion = f32[3,8,128,128]{3,2,1,0:T(8,128)S(1)} fusion(f32[1,8,32,128]{3,2,1,0:T(8,128)S(1)} %get-tuple-element.27, f32[1,8,32,128]{3,2,1,0:T(8,128)S(1)} %copy.34, f32[1,8,32,128]{3,2,1,0:T(8,128)S(1)} %get-tuple-element.26, f32[64,32]{0,1:T(8,128)S(1)} %get-tuple-element.30, f32[64,32]{0,1:T(8,128)S(1)} %get-tuple-element.31), kind=kOutput, calls=%fused_computation.4 | convolution fusion | flops 151195648 | bytes 1982464 | tf_op jit(solution)/shard_map/kn,...nm->...km/dot_general | solution.py:34
  37.7 1.4 %fusion = f32[3,8,64,256]{3,2,1,0:T(8,128)S(1)} fusion(f32[3,8,64,128]{3,2,1,0:T(8,128)S(1)} %get-tuple-element.6, f32[3,8,64,128]{3,2,1,0:T(8,128)S(1)} %get-tuple-element.5, f32[128,128]{1,0:T(8,128)S(1)} %get-tuple-element.35, f32[128,128]{1,0:T(8,128)S(1)} %fusion.47, f32[128,128]{1,0:T(8,128)S(1)} %get-tuple-element.34), kind=kOutput, calls=%fused_computation | convolution fusion | flops 1208549376 | bytes 3342336 | tf_op jit(solution)/shard_map/...n,nk->...k/dot_general | solution.py:41
  39.4 0.6 fusion.13
  40.6 3.2 %collective-permute-start = (f32[8,4096]{1,0:T(8,128)S(1)}, f32[8,4096]{1,0:T(8,128)S(1)}, u32[]{:S(2)}, u32[]{:S(2)}) collective-permute-start(f32[8,4096]{1,0:T(8,128)S(1)} %bitcast.78), channel_id=1, source_target_pairs={{0,64},{32,0},{64,32},{1,65},{33,1},{65,33},{2,66},{34,2},{66,34},... | collective-permute-start | bytes 393224 | tf_op jit(solution)/shard_map/ppermute | solution.py:85
  43.8 3.6 %collective-permute-start.1 = (f32[8,4096]{1,0:T(8,128)S(1)}, f32[8,4096]{1,0:T(8,128)S(1)}, u32[]{:S(2)}, u32[]{:S(2)}) collective-permute-start(f32[8,4096]{1,0:T(8,128)S(1)} %bitcast.79), channel_id=1, source_target_pairs={{0,32},{32,64},{64,0},{1,33},{33,65},{65,1},{2,34},{34,66},{66,2},... | collective-permute-start | bytes 393224 | tf_op jit(solution)/shard_map/ppermute | solution.py:85
  47.4 2.3 %collective-permute-done = f32[8,4096]{1,0:T(8,128)S(1)} collective-permute-done((f32[8,4096]{1,0:T(8,128)S(1)}, f32[8,4096]{1,0:T(8,128)S(1)}, u32[]{:S(2)}, u32[]{:S(2)}) %collective-permute-start) | collective-permute-done | bytes 131104 | tf_op jit(solution)/shard_map/ppermute | solution.py:85
  49.8 2.6 %collective-permute-done.1 = f32[8,4096]{1,0:T(8,128)S(1)} collective-permute-done((f32[8,4096]{1,0:T(8,128)S(1)}, f32[8,4096]{1,0:T(8,128)S(1)}, u32[]{:S(2)}, u32[]{:S(2)}) %collective-permute-start.1) | collective-permute-done | bytes 131104 | tf_op jit(solution)/shard_map/ppermute | solution.py:85
  52.5 3.5 %collective-permute-start.2 = (f32[8,4096]{1,0:T(8,128)S(1)}, f32[8,4096]{1,0:T(8,128)S(1)}, u32[]{:S(2)}, u32[]{:S(2)}) collective-permute-start(f32[8,4096]{1,0:T(8,128)S(1)} %select_add_fusion), channel_id=1, source_target_pairs={{0,96},{96,0},{192,288},{288,192},{384,480},{480,384},{576,672},{6... | collective-permute-start | bytes 393224 | tf_op jit(solution)/shard_map/ppermute | solution.py:99
  56.1 3.8 %collective-permute-done.2 = f32[8,4096]{1,0:T(8,128)S(1)} collective-permute-done((f32[8,4096]{1,0:T(8,128)S(1)}, f32[8,4096]{1,0:T(8,128)S(1)}, u32[]{:S(2)}, u32[]{:S(2)}) %collective-permute-start.2) | collective-permute-done | bytes 131104 | tf_op jit(solution)/shard_map/ppermute | solution.py:99
  59.8 4.5 %collective-permute-start.3 = (f32[8,4096]{1,0:T(8,128)S(1)}, f32[8,4096]{1,0:T(8,128)S(1)}, u32[]{:S(2)}, u32[]{:S(2)}) collective-permute-start(f32[8,4096]{1,0:T(8,128)S(1)} %add.158), channel_id=1, source_target_pairs={{0,192},{96,288},{192,0},{288,96},{384,576},{480,672},{576,384},{6... | collective-permute-start | bytes 393224 | tf_op jit(solution)/shard_map/ppermute | solution.py:99
  64.3 1.0 fusion.6
  65.3 4.7 %collective-permute-done.3 = f32[8,4096]{1,0:T(8,128)S(1)} collective-permute-done((f32[8,4096]{1,0:T(8,128)S(1)}, f32[8,4096]{1,0:T(8,128)S(1)}, u32[]{:S(2)}, u32[]{:S(2)}) %collective-permute-start.3) | collective-permute-done | bytes 131104 | tf_op jit(solution)/shard_map/ppermute | solution.py:99
  70.0 7.7 %collective-permute-start.4 = (f32[8,4096]{1,0:T(8,128)S(1)}, f32[8,4096]{1,0:T(8,128)S(1)}, u32[]{:S(2)}, u32[]{:S(2)}) collective-permute-start(f32[8,4096]{1,0:T(8,128)S(1)} %add.159), channel_id=1, source_target_pairs={{0,384},{96,480},{192,576},{288,672},{384,0},{480,96},{576,192},{6... | collective-permute-start | bytes 393224 | tf_op jit(solution)/shard_map/ppermute | solution.py:99
  78.0 0.7 fusion.4
  78.7 0.9 copy.16
  79.6 3.9 %all-to-all-start.1 = ((f32[2,32,8,128]{3,2,0,1:T(8,128)}), f32[2,32,8,128]{3,2,0,1:T(8,128)S(1)}, u32[]{:S(2)}, u32[]{:S(2)}) async-start(f32[2,32,8,128]{3,2,0,1:T(8,128)} %copy.16), calls=%async_computation.1 | async-start | bytes 524288 | tf_op jit(solution)/shard_map/all_to_all | solution.py:133
  83.4 0.6 collective-permute-done.4
  84.0 0.7 add_multiply_fusion
  84.7 17.5 %all-to-all-done.1 = f32[2,32,8,128]{3,2,0,1:T(8,128)S(1)} async-done(((f32[2,32,8,128]{3,2,0,1:T(8,128)}), f32[2,32,8,128]{3,2,0,1:T(8,128)S(1)}, u32[]{:S(2)}, u32[]{:S(2)}) %all-to-all-start.1) | async-done | bytes 262176 | tf_op jit(solution)/shard_map/all_to_all | solution.py:133
  102.2 0.8 fusion.35
  (35 shorter events, 3.3 us)
Async XLA Ops:
  0.6 17.1 %copy-start.4 = (f32[8,4096]{1,0:T(8,128)S(1)}, f32[8,4096]{1,0:T(8,128)}, u32[]{:S(2)}) copy-start(f32[8,4096]{1,0:T(8,128)} %param.9) | copy-start | bytes 393220
  2.6 33.2 %all-to-all-start = ((f32[2,32,8,128]{3,2,0,1:T(8,128)}), f32[2,32,8,128]{3,2,0,1:T(8,128)S(1)}, u32[]{:S(2)}, u32[]{:S(2)}) async-start(f32[2,32,8,128]{3,2,0,1:T(8,128)} %copy.14), calls=%async_computation | async-start | bytes 524288 | tf_op jit(solution)/shard_map/all_to_all | solution.py:128
  40.6 9.2 %collective-permute-start = (f32[8,4096]{1,0:T(8,128)S(1)}, f32[8,4096]{1,0:T(8,128)S(1)}, u32[]{:S(2)}, u32[]{:S(2)}) collective-permute-start(f32[8,4096]{1,0:T(8,128)S(1)} %bitcast.78), channel_id=1, source_target_pairs={{0,64},{32,0},{64,32},{1,65},{33,1},{65,33},{2,66},{34,2},{66,34},... | collective-permute-start | bytes 393224 | tf_op jit(solution)/shard_map/ppermute | solution.py:85
  43.8 8.6 %collective-permute-start.1 = (f32[8,4096]{1,0:T(8,128)S(1)}, f32[8,4096]{1,0:T(8,128)S(1)}, u32[]{:S(2)}, u32[]{:S(2)}) collective-permute-start(f32[8,4096]{1,0:T(8,128)S(1)} %bitcast.79), channel_id=1, source_target_pairs={{0,32},{32,64},{64,0},{1,33},{33,65},{65,1},{2,34},{34,66},{66,2},... | collective-permute-start | bytes 393224 | tf_op jit(solution)/shard_map/ppermute | solution.py:85
  52.5 7.3 %collective-permute-start.2 = (f32[8,4096]{1,0:T(8,128)S(1)}, f32[8,4096]{1,0:T(8,128)S(1)}, u32[]{:S(2)}, u32[]{:S(2)}) collective-permute-start(f32[8,4096]{1,0:T(8,128)S(1)} %select_add_fusion), channel_id=1, source_target_pairs={{0,96},{96,0},{192,288},{288,192},{384,480},{480,384},{576,672},{6... | collective-permute-start | bytes 393224 | tf_op jit(solution)/shard_map/ppermute | solution.py:99
  59.8 10.2 %collective-permute-start.3 = (f32[8,4096]{1,0:T(8,128)S(1)}, f32[8,4096]{1,0:T(8,128)S(1)}, u32[]{:S(2)}, u32[]{:S(2)}) collective-permute-start(f32[8,4096]{1,0:T(8,128)S(1)} %add.158), channel_id=1, source_target_pairs={{0,192},{96,288},{192,0},{288,96},{384,576},{480,672},{576,384},{6... | collective-permute-start | bytes 393224 | tf_op jit(solution)/shard_map/ppermute | solution.py:99
  70.0 14.0 %collective-permute-start.4 = (f32[8,4096]{1,0:T(8,128)S(1)}, f32[8,4096]{1,0:T(8,128)S(1)}, u32[]{:S(2)}, u32[]{:S(2)}) collective-permute-start(f32[8,4096]{1,0:T(8,128)S(1)} %add.159), channel_id=1, source_target_pairs={{0,384},{96,480},{192,576},{288,672},{384,0},{480,96},{576,192},{6... | collective-permute-start | bytes 393224 | tf_op jit(solution)/shard_map/ppermute | solution.py:99
  77.9 24.3 %copy-start = (f32[1,256,128]{2,1,0:T(8,128)S(1)}, f32[1,256,128]{2,1,0:T(8,128)}, u32[]{:S(2)}) copy-start(f32[1,256,128]{2,1,0:T(8,128)} %param.6) | copy-start | bytes 393220
  78.0 24.3 %copy-start.1 = (f32[1,256,128]{2,1,0:T(8,128)S(1)}, f32[1,256,128]{2,1,0:T(8,128)}, u32[]{:S(2)}) copy-start(f32[1,256,128]{2,1,0:T(8,128)} %param.8) | copy-start | bytes 393220
  78.0 24.3 %copy-start.2 = (f32[1,256,128]{2,1,0:T(8,128)S(1)}, f32[1,256,128]{2,1,0:T(8,128)}, u32[]{:S(2)}) copy-start(f32[1,256,128]{2,1,0:T(8,128)} %param.5) | copy-start | bytes 393220
  78.0 24.3 %copy-start.3 = (f32[1,256,128]{2,1,0:T(8,128)S(1)}, f32[1,256,128]{2,1,0:T(8,128)}, u32[]{:S(2)}) copy-start(f32[1,256,128]{2,1,0:T(8,128)} %param.7) | copy-start | bytes 393220
  79.6 22.6 %all-to-all-start.1 = ((f32[2,32,8,128]{3,2,0,1:T(8,128)}), f32[2,32,8,128]{3,2,0,1:T(8,128)S(1)}, u32[]{:S(2)}, u32[]{:S(2)}) async-start(f32[2,32,8,128]{3,2,0,1:T(8,128)} %copy.16), calls=%async_computation.1 | async-start | bytes 524288 | tf_op jit(solution)/shard_map/all_to_all | solution.py:133

commit v3 on v2

--- a/solution.py
+++ b/solution.py
@@ -7,7 +7,7 @@
 from jax.sharding import PartitionSpec as P
 
 
-highest = lax.Precision.HIGHEST
+matmul_precision = lax.Precision.HIGH
 
 
 def dft_tables(rows, cols, total, sign):
@@ -31,19 +31,19 @@
     held = signal.shape[-1] // minor
     blocks = signal.reshape(lead + (held, minor))
     cosine, sine = dft_tables(major, held, major, -1.0)
-    part = jnp.einsum("kn,...nm->...km", jnp.concatenate([cosine, sine], axis=0), blocks, precision=highest)
+    part = jnp.einsum("kn,...nm->...km", jnp.concatenate([cosine, sine], axis=0), blocks, precision=matmul_precision)
     part_real, part_imag = part[..., :major, :], part[..., major:, :]
     twiddle_cos, twiddle_sin = dft_tables(major, minor, padded, -1.0)
     turned = jnp.concatenate(
         [part_real * twiddle_cos - part_imag * twiddle_sin, part_real * twiddle_sin + part_imag * twiddle_cos],
         axis=-1,
     )
-    return jnp.einsum("...n,nk->...k", turned, mix_table(minor, -1.0), precision=highest)
+    return jnp.einsum("...n,nk->...k", turned, mix_table(minor, -1.0), precision=matmul_precision)
 
 
 def inverse_real(spectrum, major, minor, keep):
     padded = major * minor
-    mixed = jnp.einsum("...n,nk->...k", spectrum, mix_table(minor, 1.0), precision=highest)
+    mixed = jnp.einsum("...n,nk->...k", spectrum, mix_table(minor, 1.0), precision=matmul_precision)
     mixed_real, mixed_imag = mixed[..., :minor], mixed[..., minor:]
     twiddle_cos, twiddle_sin = dft_tables(major, minor, padded, 1.0)
     turned = jnp.concatenate(
@@ -52,7 +52,7 @@
     )
     rows = keep // minor
     cosine, sine = dft_tables(rows, major, major, 1.0)
-    out = jnp.einsum("kn,...nm->...km", jnp.concatenate([cosine, -sine], axis=1), turned, precision=highest)
+    out = jnp.einsum("kn,...nm->...km", jnp.concatenate([cosine, -sine], axis=1), turned, precision=matmul_precision)
     return out.reshape(out.shape[:-2] + (rows * minor,))
 
 
@@ -77,26 +77,42 @@
     return (both[0], both[1], filt_local)
 
 
-def sum_in_order(part, axis):
-    size = lax.axis_size(axis)
-    me = lax.axis_index(axis)
-    held = {0: part}
-    for shift in range(1, size):
-        held[shift] = lax.ppermute(part, axis, [(j, (j + shift) % size) for j in range(size)])
+def sum_first_round(part, wide, narrow):
+    size_w = lax.axis_size(wide)
+    size_n = lax.axis_size(narrow)
+    half = size_w // 2
+    y = lax.axis_index(wide)
+    z = lax.axis_index(narrow)
+    held = {}
+    for dy in (0, half):
+        for dz in range(size_n):
+            if dy == 0 and dz == 0:
+                held[(dy, dz)] = part
+                continue
+            pairs = [
+                (a * size_n + b, (a ^ dy) * size_n + (b + dz) % size_n)
+                for a in range(size_w)
+                for b in range(size_n)
+            ]
+            held[(dy, dz)] = lax.ppermute(part, (wide, narrow), pairs)
+    mine = (y // half) % 2
     total = None
-    for member in range(size):
-        value = held[0]
-        for shift in range(1, size):
-            value = jnp.where((me - shift) % size == member, held[shift], value)
-        total = value if total is None else total + value
+    for bit in range(2):
+        for zm in range(size_n):
+            value = held[(0, 0)]
+            for (dy, dz), got in held.items():
+                if dy == 0 and dz == 0:
+                    continue
+                same = (bit == mine) if dy == 0 else (bit != mine)
+                value = jnp.where(same & ((z - dz) % size_n == zm), got, value)
+            total = value if total is None else total + value
     return total
 
 
-def sum_by_doubling(part, axis):
-    size = lax.axis_size(axis)
+def sum_by_doubling(part, axis, below):
     step = 1
-    while step < size:
-        part = part + lax.ppermute(part, axis, [(j, j ^ step) for j in range(size)])
+    while step < below:
+        part = part + lax.ppermute(part, axis, [(j, j ^ step) for j in range(lax.axis_size(axis))])
         step *= 2
     return part
 
@@ -105,8 +121,8 @@
     if len(dp_axes) == 1:
         return lax.psum(part, dp_axes)
     wide, narrow = dp_axes
-    part = sum_in_order(part, narrow)
-    return sum_by_doubling(part, wide)
+    part = sum_first_round(part, wide, narrow)
+    return sum_by_doubling(part, wide, lax.axis_size(wide) // 2)
 
 
 def body(query, key_in, value, grad_out, filt, dp_axes=("dp",)):
@@ -147,7 +163,7 @@
     batches = mesh.shape["dp"]
     narrow = 3
     wide = batches // narrow
-    if batches % narrow == 0 and wide & (wide - 1) == 0:
+    if batches % narrow == 0 and wide >= 2 and wide & (wide - 1) == 0:
         devices = mesh.devices.reshape(wide, narrow, mesh.shape["seq"])
         mesh = Mesh(devices, ("dp_wide", "dp_narrow", "seq"))
         dp_axes = ("dp_wide", "dp_narrow")

time: 104 us -> 109 us (1.048)
  the two profiles are of different devices: /device:TPU:128 before, /device:TPU:1 now
where the time goes in v3:
time: 109 us
  starting transfers between devices  59.7 us (55%)
  waiting for transfers between devices  37.5 us (34%)
  other arithmetic  5.32 us (5%)
  matrix products  3.35 us (3%)
  local copies, waits for them, and re-layouts  1.97 us (2%)
  between operations  1.13 us (1%)
    ppermute x5, starting transfers between devices, sum_first_round(): held[dy, dz] = lax.ppermute(part, (wide, narrow), pairs)  28.4 us
    all_to_all x1, starting transfers between devices, body_steps(): got = lax.all_to_all(sent, 'seq', split_axis=1, concat_axis=1, tiled=True)  18.6 us
    all_to_all x1, waiting for transfers between devices, body_steps(): back = lax.all_to_all(back, 'seq', split_axis=1, concat_axis=1, tiled=True)  15.1 us
    all_to_all x1, waiting for transfers between devices, body_steps(): got = lax.all_to_all(sent, 'seq', split_axis=1, concat_axis=1, tiled=True)  12.3 us
    all_to_all x1, starting transfers between devices, body_steps(): back = lax.all_to_all(back, 'seq', split_axis=1, concat_axis=1, tiled=True)  8.87 us
    ppermute x5, waiting for transfers between devices, sum_first_round(): held[dy, dz] = lax.ppermute(part, (wide, narrow), pairs)  6.16 us
    ppermute x2, waiting for transfers between devices, sum_by_doubling(): lax.ppermute(part, axis, [(j, j ^ step) for j in range(lax.axis_size(axis...  3.94 us
    ppermute x2, starting transfers between devices, sum_by_doubling(): lax.ppermute(part, axis, [(j, j ^ step) for j in range(lax.axis_size(axis...  3.84 us
  transfers between devices with their start and end apart: 9, of which 4 were waited for; matrix products, arithmetic and copies ran while one was open for 4% of the time, Pallas kernels for 0%

profile of v3, /device:TPU:1, one launch (start us, length us, event | category | flops | bytes accessed | tf_op | source)
XLA Modules:
  0.0 109.0 jit_solution(13539296052525509553)
XLA Ops:
  0.6 1.2 %multiply_bitcast_fusion = (f32[1,32,8,128]{3,2,1,0:T(8,128)S(1)}, f32[1,32,8,128]{3,2,1,0:T(8,128)S(1)}) fusion(f32[1,256,128]{2,1,0:T(8,128)} %param.8, f32[1,256,128]{2,1,0:T(8,128)} %param.5, f32[1,256,128]{2,1,0:T(8,128)} %param.6, f32[1,256,128]{2,1,0:T(8,128)} %param.7), kind=kLoop, calls=%fused_computation.63 | loop fusion | flops 65536 | bytes 786432 | tf_op jit(solution)/shard_map/stack | solution.py:143
  1.8 0.7 copy.14
  2.6 18.6 %all-to-all-start = ((f32[2,32,8,128]{3,2,0,1:T(8,128)}), f32[2,32,8,128]{3,2,0,1:T(8,128)S(1)}, u32[]{:S(2)}, u32[]{:S(2)}) async-start(f32[2,32,8,128]{3,2,0,1:T(8,128)} %copy.14), calls=%async_computation | async-start | bytes 524288 | tf_op jit(solution)/shard_map/all_to_all | solution.py:144
  22.9 12.3 %all-to-all-done = f32[2,32,8,128]{3,2,0,1:T(8,128)S(1)} async-done(((f32[2,32,8,128]{3,2,0,1:T(8,128)}), f32[2,32,8,128]{3,2,0,1:T(8,128)S(1)}, u32[]{:S(2)}, u32[]{:S(2)}) %all-to-all-start) | async-done | bytes 262176 | tf_op jit(solution)/shard_map/all_to_all | solution.py:144
  35.4 0.9 convolution_bitcast_fusion
  36.6 0.8 fusion
  37.7 0.4 fusion.13
  38.6 13.3 %collective-permute-start = (f32[8,4096]{1,0:T(8,128)S(1)}, f32[8,4096]{1,0:T(8,128)S(1)}, u32[]{:S(2)}, u32[]{:S(2)}) collective-permute-start(f32[8,4096]{1,0:T(8,128)S(1)} %bitcast.78), channel_id=1, source_target_pairs={{0,448},{32,384},{64,416},{96,544},{128,480},{160,512},{192,640},{... | collective-permute-start | bytes 393224 | tf_op jit(solution)/shard_map/ppermute | solution.py:97
  51.9 1.9 %collective-permute-start.1 = (f32[8,4096]{1,0:T(8,128)S(1)}, f32[8,4096]{1,0:T(8,128)S(1)}, u32[]{:S(2)}, u32[]{:S(2)}) collective-permute-start(f32[8,4096]{1,0:T(8,128)S(1)} %bitcast.79), channel_id=1, source_target_pairs={{0,416},{32,448},{64,384},{96,512},{128,544},{160,480},{192,608},{... | collective-permute-start | bytes 393224 | tf_op jit(solution)/shard_map/ppermute | solution.py:97
  53.8 2.3 %collective-permute-start.2 = (f32[8,4096]{1,0:T(8,128)S(1)}, f32[8,4096]{1,0:T(8,128)S(1)}, u32[]{:S(2)}, u32[]{:S(2)}) collective-permute-start(f32[8,4096]{1,0:T(8,128)S(1)} %bitcast.80), channel_id=1, source_target_pairs={{0,384},{32,416},{64,448},{96,480},{128,512},{160,544},{192,576},{... | collective-permute-start | bytes 393224 | tf_op jit(solution)/shard_map/ppermute | solution.py:97
  56.1 9.0 %collective-permute-start.3 = (f32[8,4096]{1,0:T(8,128)S(1)}, f32[8,4096]{1,0:T(8,128)S(1)}, u32[]{:S(2)}, u32[]{:S(2)}) collective-permute-start(f32[8,4096]{1,0:T(8,128)S(1)} %bitcast.81), channel_id=1, source_target_pairs={{0,64},{32,0},{64,32},{96,160},{128,96},{160,128},{192,256},{224,1... | collective-permute-start | bytes 393224 | tf_op jit(solution)/shard_map/ppermute | solution.py:97
  65.1 1.9 %collective-permute-start.4 = (f32[8,4096]{1,0:T(8,128)S(1)}, f32[8,4096]{1,0:T(8,128)S(1)}, u32[]{:S(2)}, u32[]{:S(2)}) collective-permute-start(f32[8,4096]{1,0:T(8,128)S(1)} %bitcast.82), channel_id=1, source_target_pairs={{0,32},{32,64},{64,0},{96,128},{128,160},{160,96},{192,224},{224,2... | collective-permute-start | bytes 393224 | tf_op jit(solution)/shard_map/ppermute | solution.py:97
  67.2 6.1 %collective-permute-done.2 = f32[8,4096]{1,0:T(8,128)S(1)} collective-permute-done((f32[8,4096]{1,0:T(8,128)S(1)}, f32[8,4096]{1,0:T(8,128)S(1)}, u32[]{:S(2)}, u32[]{:S(2)}) %collective-permute-start.2) | collective-permute-done | bytes 131104 | tf_op jit(solution)/shard_map/ppermute | solution.py:97
  73.4 0.3 select_add_fusion
  73.7 1.9 %collective-permute-start.5 = (f32[8,4096]{1,0:T(8,128)S(1)}, f32[8,4096]{1,0:T(8,128)S(1)}, u32[]{:S(2)}, u32[]{:S(2)}) collective-permute-start(f32[8,4096]{1,0:T(8,128)S(1)} %select_add_fusion), channel_id=1, source_target_pairs={{0,96},{96,0},{192,288},{288,192},{384,480},{480,384},{576,672},{6... | collective-permute-start | bytes 393224 | tf_op jit(solution)/shard_map/ppermute | solution.py:115
  75.6 0.6 fusion.6
  76.2 3.9 %collective-permute-done.5 = f32[8,4096]{1,0:T(8,128)S(1)} collective-permute-done((f32[8,4096]{1,0:T(8,128)S(1)}, f32[8,4096]{1,0:T(8,128)S(1)}, u32[]{:S(2)}, u32[]{:S(2)}) %collective-permute-start.5) | collective-permute-done | bytes 131104 | tf_op jit(solution)/shard_map/ppermute | solution.py:115
  80.1 1.9 %collective-permute-start.6 = (f32[8,4096]{1,0:T(8,128)S(1)}, f32[8,4096]{1,0:T(8,128)S(1)}, u32[]{:S(2)}, u32[]{:S(2)}) collective-permute-start(f32[8,4096]{1,0:T(8,128)S(1)} %add.199), channel_id=1, source_target_pairs={{0,192},{96,288},{192,0},{288,96},{384,576},{480,672},{576,384},{6... | collective-permute-start | bytes 393224 | tf_op jit(solution)/shard_map/ppermute | solution.py:115
  82.3 0.4 fusion.4
  82.7 0.9 copy.16
  83.5 8.9 %all-to-all-start.1 = ((f32[2,32,8,128]{3,2,0,1:T(8,128)}), f32[2,32,8,128]{3,2,0,1:T(8,128)S(1)}, u32[]{:S(2)}, u32[]{:S(2)}) async-start(f32[2,32,8,128]{3,2,0,1:T(8,128)} %copy.16), calls=%async_computation.1 | async-start | bytes 524288 | tf_op jit(solution)/shard_map/all_to_all | solution.py:149
  92.4 0.7 add_multiply_fusion
  93.1 15.1 %all-to-all-done.1 = f32[2,32,8,128]{3,2,0,1:T(8,128)S(1)} async-done(((f32[2,32,8,128]{3,2,0,1:T(8,128)}), f32[2,32,8,128]{3,2,0,1:T(8,128)S(1)}, u32[]{:S(2)}, u32[]{:S(2)}) %all-to-all-start.1) | async-done | bytes 262176 | tf_op jit(solution)/shard_map/all_to_all | solution.py:149
  108.2 0.8 fusion.35
  (38 shorter events, 3.1 us)
Async XLA Ops:
  0.6 20.8 %copy-start.4 = (f32[8,4096]{1,0:T(8,128)S(1)}, f32[8,4096]{1,0:T(8,128)}, u32[]{:S(2)}) copy-start(f32[8,4096]{1,0:T(8,128)} %param.9) | copy-start | bytes 393220
  2.6 32.7 %all-to-all-start = ((f32[2,32,8,128]{3,2,0,1:T(8,128)}), f32[2,32,8,128]{3,2,0,1:T(8,128)S(1)}, u32[]{:S(2)}, u32[]{:S(2)}) async-start(f32[2,32,8,128]{3,2,0,1:T(8,128)} %copy.14), calls=%async_computation | async-start | bytes 524288 | tf_op jit(solution)/shard_map/all_to_all | solution.py:144
  38.6 28.6 %collective-permute-start = (f32[8,4096]{1,0:T(8,128)S(1)}, f32[8,4096]{1,0:T(8,128)S(1)}, u32[]{:S(2)}, u32[]{:S(2)}) collective-permute-start(f32[8,4096]{1,0:T(8,128)S(1)} %bitcast.78), channel_id=1, source_target_pairs={{0,448},{32,384},{64,416},{96,544},{128,480},{160,512},{192,640},{... | collective-permute-start | bytes 393224 | tf_op jit(solution)/shard_map/ppermute | solution.py:97
  51.9 15.3 %collective-permute-start.1 = (f32[8,4096]{1,0:T(8,128)S(1)}, f32[8,4096]{1,0:T(8,128)S(1)}, u32[]{:S(2)}, u32[]{:S(2)}) collective-permute-start(f32[8,4096]{1,0:T(8,128)S(1)} %bitcast.79), channel_id=1, source_target_pairs={{0,416},{32,448},{64,384},{96,512},{128,544},{160,480},{192,608},{... | collective-permute-start | bytes 393224 | tf_op jit(solution)/shard_map/ppermute | solution.py:97
  53.8 19.5 %collective-permute-start.2 = (f32[8,4096]{1,0:T(8,128)S(1)}, f32[8,4096]{1,0:T(8,128)S(1)}, u32[]{:S(2)}, u32[]{:S(2)}) collective-permute-start(f32[8,4096]{1,0:T(8,128)S(1)} %bitcast.80), channel_id=1, source_target_pairs={{0,384},{32,416},{64,448},{96,480},{128,512},{160,544},{192,576},{... | collective-permute-start | bytes 393224 | tf_op jit(solution)/shard_map/ppermute | solution.py:97
  56.1 17.2 %collective-permute-start.3 = (f32[8,4096]{1,0:T(8,128)S(1)}, f32[8,4096]{1,0:T(8,128)S(1)}, u32[]{:S(2)}, u32[]{:S(2)}) collective-permute-start(f32[8,4096]{1,0:T(8,128)S(1)} %bitcast.81), channel_id=1, source_target_pairs={{0,64},{32,0},{64,32},{96,160},{128,96},{160,128},{192,256},{224,1... | collective-permute-start | bytes 393224 | tf_op jit(solution)/shard_map/ppermute | solution.py:97
  65.1 8.3 %collective-permute-start.4 = (f32[8,4096]{1,0:T(8,128)S(1)}, f32[8,4096]{1,0:T(8,128)S(1)}, u32[]{:S(2)}, u32[]{:S(2)}) collective-permute-start(f32[8,4096]{1,0:T(8,128)S(1)} %bitcast.82), channel_id=1, source_target_pairs={{0,32},{32,64},{64,0},{96,128},{128,160},{160,96},{192,224},{224,2... | collective-permute-start | bytes 393224 | tf_op jit(solution)/shard_map/ppermute | solution.py:97
  73.7 6.5 %collective-permute-start.5 = (f32[8,4096]{1,0:T(8,128)S(1)}, f32[8,4096]{1,0:T(8,128)S(1)}, u32[]{:S(2)}, u32[]{:S(2)}) collective-permute-start(f32[8,4096]{1,0:T(8,128)S(1)} %select_add_fusion), channel_id=1, source_target_pairs={{0,96},{96,0},{192,288},{288,192},{384,480},{480,384},{576,672},{6... | collective-permute-start | bytes 393224 | tf_op jit(solution)/shard_map/ppermute | solution.py:115
  80.1 12.3 %collective-permute-start.6 = (f32[8,4096]{1,0:T(8,128)S(1)}, f32[8,4096]{1,0:T(8,128)S(1)}, u32[]{:S(2)}, u32[]{:S(2)}) collective-permute-start(f32[8,4096]{1,0:T(8,128)S(1)} %add.199), channel_id=1, source_target_pairs={{0,192},{96,288},{192,0},{288,96},{384,576},{480,672},{576,384},{6... | collective-permute-start | bytes 393224 | tf_op jit(solution)/shard_map/ppermute | solution.py:115
  82.2 26.0 %copy-start = (f32[1,256,128]{2,1,0:T(8,128)S(1)}, f32[1,256,128]{2,1,0:T(8,128)}, u32[]{:S(2)}) copy-start(f32[1,256,128]{2,1,0:T(8,128)} %param.6) | copy-start | bytes 393220
  82.2 26.0 %copy-start.1 = (f32[1,256,128]{2,1,0:T(8,128)S(1)}, f32[1,256,128]{2,1,0:T(8,128)}, u32[]{:S(2)}) copy-start(f32[1,256,128]{2,1,0:T(8,128)} %param.8) | copy-start | bytes 393220
  82.2 25.9 %copy-start.2 = (f32[1,256,128]{2,1,0:T(8,128)S(1)}, f32[1,256,128]{2,1,0:T(8,128)}, u32[]{:S(2)}) copy-start(f32[1,256,128]{2,1,0:T(8,128)} %param.5) | copy-start | bytes 393220
  82.3 25.9 %copy-start.3 = (f32[1,256,128]{2,1,0:T(8,128)S(1)}, f32[1,256,128]{2,1,0:T(8,128)}, u32[]{:S(2)}) copy-start(f32[1,256,128]{2,1,0:T(8,128)} %param.7) | copy-start | bytes 393220
  83.5 24.6 %all-to-all-start.1 = ((f32[2,32,8,128]{3,2,0,1:T(8,128)}), f32[2,32,8,128]{3,2,0,1:T(8,128)S(1)}, u32[]{:S(2)}, u32[]{:S(2)}) async-start(f32[2,32,8,128]{3,2,0,1:T(8,128)} %copy.16), calls=%async_computation.1 | async-start | bytes 524288 | tf_op jit(solution)/shard_map/all_to_all | solution.py:149

commit v4 on v2

--- a/solution.py
+++ b/solution.py
@@ -7,7 +7,7 @@
 from jax.sharding import PartitionSpec as P
 
 
-highest = lax.Precision.HIGHEST
+matmul_precision = lax.Precision.HIGH
 
 
 def dft_tables(rows, cols, total, sign):
@@ -31,19 +31,19 @@
     held = signal.shape[-1] // minor
     blocks = signal.reshape(lead + (held, minor))
     cosine, sine = dft_tables(major, held, major, -1.0)
-    part = jnp.einsum("kn,...nm->...km", jnp.concatenate([cosine, sine], axis=0), blocks, precision=highest)
+    part = jnp.einsum("kn,...nm->...km", jnp.concatenate([cosine, sine], axis=0), blocks, precision=matmul_precision)
     part_real, part_imag = part[..., :major, :], part[..., major:, :]
     twiddle_cos, twiddle_sin = dft_tables(major, minor, padded, -1.0)
     turned = jnp.concatenate(
         [part_real * twiddle_cos - part_imag * twiddle_sin, part_real * twiddle_sin + part_imag * twiddle_cos],
         axis=-1,
     )
-    return jnp.einsum("...n,nk->...k", turned, mix_table(minor, -1.0), precision=highest)
+    return jnp.einsum("...n,nk->...k", turned, mix_table(minor, -1.0), precision=matmul_precision)
 
 
 def inverse_real(spectrum, major, minor, keep):
     padded = major * minor
-    mixed = jnp.einsum("...n,nk->...k", spectrum, mix_table(minor, 1.0), precision=highest)
+    mixed = jnp.einsum("...n,nk->...k", spectrum, mix_table(minor, 1.0), precision=matmul_precision)
     mixed_real, mixed_imag = mixed[..., :minor], mixed[..., minor:]
     twiddle_cos, twiddle_sin = dft_tables(major, minor, padded, 1.0)
     turned = jnp.concatenate(
@@ -52,7 +52,7 @@
     )
     rows = keep // minor
     cosine, sine = dft_tables(rows, major, major, 1.0)
-    out = jnp.einsum("kn,...nm->...km", jnp.concatenate([cosine, -sine], axis=1), turned, precision=highest)
+    out = jnp.einsum("kn,...nm->...km", jnp.concatenate([cosine, -sine], axis=1), turned, precision=matmul_precision)
     return out.reshape(out.shape[:-2] + (rows * minor,))
 
 

time: 104 us -> 102 us (0.981)
  matrix products: 5.58 us -> 3.34 us
    dot_general x3, matrix products: 2.96 us -> 1.76 us  [the longest x2 0.96 us: inverse_real(): jnp.einsum('...n,nk->...k', spectrum, mix_table(minor, 1.0), precision=ma...]
  transfers between devices with their start and end apart: 7 -> 7, of which waited for: 7 -> 7; matrix products, arithmetic and copies ran while one was open for 5% -> 4% of each run, Pallas kernels for 0% -> 0%
where the time goes in v4:
time: 102 us; the launch traced here: 101 us
  waiting for transfers between devices  48.4 us (47%)
  starting transfers between devices  41.3 us (40%)
  other arithmetic  5.14 us (5%)
  matrix products  3.34 us (3%)
  local copies, waits for them, and re-layouts  1.99 us (2%)
    all_to_all x1, waiting for transfers between devices, body_steps(): back = lax.all_to_all(back, 'seq', split_axis=1, concat_axis=1, tiled=True)  17.2 us
    all_to_all x1, waiting for transfers between devices, body_steps(): got = lax.all_to_all(sent, 'seq', split_axis=1, concat_axis=1, tiled=True)  16.5 us
    ppermute x3, starting transfers between devices, sum_by_doubling(): part = part + lax.ppermute(part, axis, [(j, j ^ step) for j in range(size)])  15.7 us
    all_to_all x1, starting transfers between devices, body_steps(): got = lax.all_to_all(sent, 'seq', split_axis=1, concat_axis=1, tiled=True)  15 us
    ppermute x3, waiting for transfers between devices, sum_by_doubling(): part = part + lax.ppermute(part, axis, [(j, j ^ step) for j in range(size)])  9.71 us
    ppermute x2, starting transfers between devices, sum_in_order(): lax.ppermute(part, axis, [(j, (j + shift) % size) for j in range(size)])  6.74 us
    ppermute x2, waiting for transfers between devices, sum_in_order(): lax.ppermute(part, axis, [(j, (j + shift) % size) for j in range(size)])  4.94 us
    all_to_all x1, starting transfers between devices, body_steps(): back = lax.all_to_all(back, 'seq', split_axis=1, concat_axis=1, tiled=True)  3.87 us
  transfers between devices with their start and end apart: 7, of which 7 were waited for; matrix products, arithmetic and copies ran while one was open for 4% of the time, Pallas kernels for 0%

profile of v4, /device:TPU:128, one launch (start us, length us, event | category | flops | bytes accessed | tf_op | source)
XLA Modules:
  0.0 101.2 jit_solution(12293312042704348721)
XLA Ops:
  0.6 1.2 %multiply_bitcast_fusion = (f32[1,32,8,128]{3,2,1,0:T(8,128)S(1)}, f32[1,32,8,128]{3,2,1,0:T(8,128)S(1)}) fusion(f32[1,256,128]{2,1,0:T(8,128)} %param.8, f32[1,256,128]{2,1,0:T(8,128)} %param.5, f32[1,256,128]{2,1,0:T(8,128)} %param.6, f32[1,256,128]{2,1,0:T(8,128)} %param.7), kind=kLoop, calls=%fused_computation.63 | loop fusion | flops 65536 | bytes 786432 | tf_op jit(solution)/shard_map/stack | solution.py:127
  1.8 0.7 copy.14
  2.6 15.0 %all-to-all-start = ((f32[2,32,8,128]{3,2,0,1:T(8,128)}), f32[2,32,8,128]{3,2,0,1:T(8,128)S(1)}, u32[]{:S(2)}, u32[]{:S(2)}) async-start(f32[2,32,8,128]{3,2,0,1:T(8,128)} %copy.14), calls=%async_computation | async-start | bytes 524288 | tf_op jit(solution)/shard_map/all_to_all | solution.py:128
  19.2 16.5 %all-to-all-done = f32[2,32,8,128]{3,2,0,1:T(8,128)S(1)} async-done(((f32[2,32,8,128]{3,2,0,1:T(8,128)}), f32[2,32,8,128]{3,2,0,1:T(8,128)S(1)}, u32[]{:S(2)}, u32[]{:S(2)}) %all-to-all-start) | async-done | bytes 262176 | tf_op jit(solution)/shard_map/all_to_all | solution.py:128
  35.9 0.9 convolution_bitcast_fusion
  37.1 0.8 fusion
  38.2 0.4 fusion.13
  39.1 3.2 %collective-permute-start = (f32[8,4096]{1,0:T(8,128)S(1)}, f32[8,4096]{1,0:T(8,128)S(1)}, u32[]{:S(2)}, u32[]{:S(2)}) collective-permute-start(f32[8,4096]{1,0:T(8,128)S(1)} %bitcast.78), channel_id=1, source_target_pairs={{0,64},{32,0},{64,32},{1,65},{33,1},{65,33},{2,66},{34,2},{66,34},... | collective-permute-start | bytes 393224 | tf_op jit(solution)/shard_map/ppermute | solution.py:85
  42.2 3.6 %collective-permute-start.1 = (f32[8,4096]{1,0:T(8,128)S(1)}, f32[8,4096]{1,0:T(8,128)S(1)}, u32[]{:S(2)}, u32[]{:S(2)}) collective-permute-start(f32[8,4096]{1,0:T(8,128)S(1)} %bitcast.79), channel_id=1, source_target_pairs={{0,32},{32,64},{64,0},{1,33},{33,65},{65,1},{2,34},{34,66},{66,2},... | collective-permute-start | bytes 393224 | tf_op jit(solution)/shard_map/ppermute | solution.py:85
  45.9 2.3 %collective-permute-done = f32[8,4096]{1,0:T(8,128)S(1)} collective-permute-done((f32[8,4096]{1,0:T(8,128)S(1)}, f32[8,4096]{1,0:T(8,128)S(1)}, u32[]{:S(2)}, u32[]{:S(2)}) %collective-permute-start) | collective-permute-done | bytes 131104 | tf_op jit(solution)/shard_map/ppermute | solution.py:85
  48.2 2.6 %collective-permute-done.1 = f32[8,4096]{1,0:T(8,128)S(1)} collective-permute-done((f32[8,4096]{1,0:T(8,128)S(1)}, f32[8,4096]{1,0:T(8,128)S(1)}, u32[]{:S(2)}, u32[]{:S(2)}) %collective-permute-start.1) | collective-permute-done | bytes 131104 | tf_op jit(solution)/shard_map/ppermute | solution.py:85
  50.9 3.5 %collective-permute-start.2 = (f32[8,4096]{1,0:T(8,128)S(1)}, f32[8,4096]{1,0:T(8,128)S(1)}, u32[]{:S(2)}, u32[]{:S(2)}) collective-permute-start(f32[8,4096]{1,0:T(8,128)S(1)} %select_add_fusion), channel_id=1, source_target_pairs={{0,96},{96,0},{192,288},{288,192},{384,480},{480,384},{576,672},{6... | collective-permute-start | bytes 393224 | tf_op jit(solution)/shard_map/ppermute | solution.py:99
  54.5 3.8 %collective-permute-done.2 = f32[8,4096]{1,0:T(8,128)S(1)} collective-permute-done((f32[8,4096]{1,0:T(8,128)S(1)}, f32[8,4096]{1,0:T(8,128)S(1)}, u32[]{:S(2)}, u32[]{:S(2)}) %collective-permute-start.2) | collective-permute-done | bytes 131104 | tf_op jit(solution)/shard_map/ppermute | solution.py:99
  58.3 4.5 %collective-permute-start.3 = (f32[8,4096]{1,0:T(8,128)S(1)}, f32[8,4096]{1,0:T(8,128)S(1)}, u32[]{:S(2)}, u32[]{:S(2)}) collective-permute-start(f32[8,4096]{1,0:T(8,128)S(1)} %add.158), channel_id=1, source_target_pairs={{0,192},{96,288},{192,0},{288,96},{384,576},{480,672},{576,384},{6... | collective-permute-start | bytes 393224 | tf_op jit(solution)/shard_map/ppermute | solution.py:99
  62.8 0.6 fusion.6
  63.4 5.1 %collective-permute-done.3 = f32[8,4096]{1,0:T(8,128)S(1)} collective-permute-done((f32[8,4096]{1,0:T(8,128)S(1)}, f32[8,4096]{1,0:T(8,128)S(1)}, u32[]{:S(2)}, u32[]{:S(2)}) %collective-permute-start.3) | collective-permute-done | bytes 131104 | tf_op jit(solution)/shard_map/ppermute | solution.py:99
  68.5 7.7 %collective-permute-start.4 = (f32[8,4096]{1,0:T(8,128)S(1)}, f32[8,4096]{1,0:T(8,128)S(1)}, u32[]{:S(2)}, u32[]{:S(2)}) collective-permute-start(f32[8,4096]{1,0:T(8,128)S(1)} %add.159), channel_id=1, source_target_pairs={{0,384},{96,480},{192,576},{288,672},{384,0},{480,96},{576,192},{6... | collective-permute-start | bytes 393224 | tf_op jit(solution)/shard_map/ppermute | solution.py:99
  76.4 0.4 fusion.4
  76.9 0.9 copy.16
  77.7 3.9 %all-to-all-start.1 = ((f32[2,32,8,128]{3,2,0,1:T(8,128)}), f32[2,32,8,128]{3,2,0,1:T(8,128)S(1)}, u32[]{:S(2)}, u32[]{:S(2)}) async-start(f32[2,32,8,128]{3,2,0,1:T(8,128)} %copy.16), calls=%async_computation.1 | async-start | bytes 524288 | tf_op jit(solution)/shard_map/all_to_all | solution.py:133
  81.6 0.9 collective-permute-done.4
  82.5 0.7 add_multiply_fusion
  83.1 17.2 %all-to-all-done.1 = f32[2,32,8,128]{3,2,0,1:T(8,128)S(1)} async-done(((f32[2,32,8,128]{3,2,0,1:T(8,128)}), f32[2,32,8,128]{3,2,0,1:T(8,128)S(1)}, u32[]{:S(2)}, u32[]{:S(2)}) %all-to-all-start.1) | async-done | bytes 262176 | tf_op jit(solution)/shard_map/all_to_all | solution.py:133
  100.4 0.8 fusion.35
  (35 shorter events, 3.2 us)
Async XLA Ops:
  0.6 17.1 %copy-start.4 = (f32[8,4096]{1,0:T(8,128)S(1)}, f32[8,4096]{1,0:T(8,128)}, u32[]{:S(2)}) copy-start(f32[8,4096]{1,0:T(8,128)} %param.9) | copy-start | bytes 393220
  2.6 33.2 %all-to-all-start = ((f32[2,32,8,128]{3,2,0,1:T(8,128)}), f32[2,32,8,128]{3,2,0,1:T(8,128)S(1)}, u32[]{:S(2)}, u32[]{:S(2)}) async-start(f32[2,32,8,128]{3,2,0,1:T(8,128)} %copy.14), calls=%async_computation | async-start | bytes 524288 | tf_op jit(solution)/shard_map/all_to_all | solution.py:128
  39.1 9.2 %collective-permute-start = (f32[8,4096]{1,0:T(8,128)S(1)}, f32[8,4096]{1,0:T(8,128)S(1)}, u32[]{:S(2)}, u32[]{:S(2)}) collective-permute-start(f32[8,4096]{1,0:T(8,128)S(1)} %bitcast.78), channel_id=1, source_target_pairs={{0,64},{32,0},{64,32},{1,65},{33,1},{65,33},{2,66},{34,2},{66,34},... | collective-permute-start | bytes 393224 | tf_op jit(solution)/shard_map/ppermute | solution.py:85
  42.2 8.6 %collective-permute-start.1 = (f32[8,4096]{1,0:T(8,128)S(1)}, f32[8,4096]{1,0:T(8,128)S(1)}, u32[]{:S(2)}, u32[]{:S(2)}) collective-permute-start(f32[8,4096]{1,0:T(8,128)S(1)} %bitcast.79), channel_id=1, source_target_pairs={{0,32},{32,64},{64,0},{1,33},{33,65},{65,1},{2,34},{34,66},{66,2},... | collective-permute-start | bytes 393224 | tf_op jit(solution)/shard_map/ppermute | solution.py:85
  50.9 7.3 %collective-permute-start.2 = (f32[8,4096]{1,0:T(8,128)S(1)}, f32[8,4096]{1,0:T(8,128)S(1)}, u32[]{:S(2)}, u32[]{:S(2)}) collective-permute-start(f32[8,4096]{1,0:T(8,128)S(1)} %select_add_fusion), channel_id=1, source_target_pairs={{0,96},{96,0},{192,288},{288,192},{384,480},{480,384},{576,672},{6... | collective-permute-start | bytes 393224 | tf_op jit(solution)/shard_map/ppermute | solution.py:99
  58.3 10.2 %collective-permute-start.3 = (f32[8,4096]{1,0:T(8,128)S(1)}, f32[8,4096]{1,0:T(8,128)S(1)}, u32[]{:S(2)}, u32[]{:S(2)}) collective-permute-start(f32[8,4096]{1,0:T(8,128)S(1)} %add.158), channel_id=1, source_target_pairs={{0,192},{96,288},{192,0},{288,96},{384,576},{480,672},{576,384},{6... | collective-permute-start | bytes 393224 | tf_op jit(solution)/shard_map/ppermute | solution.py:99
  68.5 14.0 %collective-permute-start.4 = (f32[8,4096]{1,0:T(8,128)S(1)}, f32[8,4096]{1,0:T(8,128)S(1)}, u32[]{:S(2)}, u32[]{:S(2)}) collective-permute-start(f32[8,4096]{1,0:T(8,128)S(1)} %add.159), channel_id=1, source_target_pairs={{0,384},{96,480},{192,576},{288,672},{384,0},{480,96},{576,192},{6... | collective-permute-start | bytes 393224 | tf_op jit(solution)/shard_map/ppermute | solution.py:99
  76.4 24.0 %copy-start = (f32[1,256,128]{2,1,0:T(8,128)S(1)}, f32[1,256,128]{2,1,0:T(8,128)}, u32[]{:S(2)}) copy-start(f32[1,256,128]{2,1,0:T(8,128)} %param.6) | copy-start | bytes 393220
  76.4 24.0 %copy-start.1 = (f32[1,256,128]{2,1,0:T(8,128)S(1)}, f32[1,256,128]{2,1,0:T(8,128)}, u32[]{:S(2)}) copy-start(f32[1,256,128]{2,1,0:T(8,128)} %param.8) | copy-start | bytes 393220
  76.4 24.0 %copy-start.2 = (f32[1,256,128]{2,1,0:T(8,128)S(1)}, f32[1,256,128]{2,1,0:T(8,128)}, u32[]{:S(2)}) copy-start(f32[1,256,128]{2,1,0:T(8,128)} %param.5) | copy-start | bytes 393220
  76.4 24.0 %copy-start.3 = (f32[1,256,128]{2,1,0:T(8,128)S(1)}, f32[1,256,128]{2,1,0:T(8,128)}, u32[]{:S(2)}) copy-start(f32[1,256,128]{2,1,0:T(8,128)} %param.7) | copy-start | bytes 393220
  77.7 22.6 %all-to-all-start.1 = ((f32[2,32,8,128]{3,2,0,1:T(8,128)}), f32[2,32,8,128]{3,2,0,1:T(8,128)S(1)}, u32[]{:S(2)}, u32[]{:S(2)}) async-start(f32[2,32,8,128]{3,2,0,1:T(8,128)} %copy.16), calls=%async_computation.1 | async-start | bytes 524288 | tf_op jit(solution)/shard_map/all_to_all | solution.py:133

commit v5 on v4

--- a/solution.py
+++ b/solution.py
@@ -7,7 +7,7 @@
 from jax.sharding import PartitionSpec as P
 
 
-matmul_precision = lax.Precision.HIGH
+matmul_precision = lax.Precision.HIGHEST
 
 
 def dft_tables(rows, cols, total, sign):
@@ -69,8 +69,9 @@
     padded = 2 * length
     minor = 128
     major = padded // minor
-    spec = forward(jnp.stack([gated, filt, grad_conv]), major, minor)
-    g_spec, f_spec, d_spec = spec[0], spec[1], spec[2]
+    f_spec = forward(filt, major, minor)
+    spec = forward(jnp.stack([gated, grad_conv]), major, minor)
+    g_spec, d_spec = spec[0], spec[1]
     pair = jnp.stack([times(f_spec, g_spec, minor, False), times(f_spec, d_spec, minor, True)])
     both = inverse_real(pair, major, minor, length) / padded
     filt_local = inverse_real(times(g_spec, d_spec, minor, True), major, minor, length) / padded

time: 102 us -> 103 us (level)
  matrix products: 3.34 us -> 6.03 us
  waiting for transfers between devices: 48.4 us -> 46.7 us
    all_to_all x1, waiting for transfers between devices: 16.5 us -> 15.2 us  [body_steps(): got = lax.all_to_all(sent, 'seq', split_axis=1, concat_axis=1, tiled=True)]
  transfers between devices with their start and end apart: 7 -> 7, of which waited for: 7 -> 7; matrix products, arithmetic and copies ran while one was open for 4% -> 6% of each run, Pallas kernels for 0% -> 0%
where the time goes in v5:
time: 103 us; the launch traced here: 102 us
  waiting for transfers between devices  46.7 us (45%)
  starting transfers between devices  41.4 us (40%)
  matrix products  6.03 us (6%)
  other arithmetic  5.08 us (5%)
  local copies, waits for them, and re-layouts  1.81 us (2%)
    all_to_all x1, waiting for transfers between devices, body_steps(): back = lax.all_to_all(back, 'seq', split_axis=1, concat_axis=1, tiled=True)  17.6 us
    ppermute x3, starting transfers between devices, sum_by_doubling(): part = part + lax.ppermute(part, axis, [(j, j ^ step) for j in range(size)])  15.7 us
    all_to_all x1, waiting for transfers between devices, body_steps(): got = lax.all_to_all(sent, 'seq', split_axis=1, concat_axis=1, tiled=True)  15.2 us
    all_to_all x1, starting transfers between devices, body_steps(): got = lax.all_to_all(sent, 'seq', split_axis=1, concat_axis=1, tiled=True)  15 us
    ppermute x3, waiting for transfers between devices, sum_by_doubling(): part = part + lax.ppermute(part, axis, [(j, j ^ step) for j in range(size)])  8.9 us
    ppermute x2, starting transfers between devices, sum_in_order(): lax.ppermute(part, axis, [(j, (j + shift) % size) for j in range(size)])  6.74 us
    ppermute x2, waiting for transfers between devices, sum_in_order(): lax.ppermute(part, axis, [(j, (j + shift) % size) for j in range(size)])  4.95 us
    all_to_all x1, starting transfers between devices, body_steps(): back = lax.all_to_all(back, 'seq', split_axis=1, concat_axis=1, tiled=True)  4 us
  transfers between devices with their start and end apart: 7, of which 7 were waited for; matrix products, arithmetic and copies ran while one was open for 6% of the time, Pallas kernels for 0%

profile of v5, /device:TPU:128, one launch (start us, length us, event | category | flops | bytes accessed | tf_op | source)
XLA Modules:
  0.0 102.0 jit_solution(5815215215751487824)
XLA Ops:
  0.6 1.2 %multiply_bitcast_fusion = (f32[1,32,8,128]{3,2,1,0:T(8,128)S(1)}, f32[1,32,8,128]{3,2,1,0:T(8,128)S(1)}) fusion(f32[1,256,128]{2,1,0:T(8,128)} %param.8, f32[1,256,128]{2,1,0:T(8,128)} %param.5, f32[1,256,128]{2,1,0:T(8,128)} %param.6, f32[1,256,128]{2,1,0:T(8,128)} %param.7), kind=kLoop, calls=%fused_computation.61 | loop fusion | flops 65536 | bytes 786432 | tf_op jit(solution)/shard_map/stack | solution.py:128
  1.8 0.7 copy.17
  2.6 15.0 %all-to-all-start = ((f32[2,32,8,128]{3,2,0,1:T(8,128)}), f32[2,32,8,128]{3,2,0,1:T(8,128)S(1)}, u32[]{:S(2)}, u32[]{:S(2)}) async-start(f32[2,32,8,128]{3,2,0,1:T(8,128)} %copy.17), calls=%async_computation | async-start | bytes 524288 | tf_op jit(solution)/shard_map/all_to_all | solution.py:129
  19.2 0.7 convolution_bitcast_fusion.1
  20.6 15.2 %all-to-all-done = f32[2,32,8,128]{3,2,0,1:T(8,128)S(1)} async-done(((f32[2,32,8,128]{3,2,0,1:T(8,128)}), f32[2,32,8,128]{3,2,0,1:T(8,128)S(1)}, u32[]{:S(2)}, u32[]{:S(2)}) %all-to-all-start) | async-done | bytes 262176 | tf_op jit(solution)/shard_map/all_to_all | solution.py:129
  35.8 1.1 %convolution_bitcast_fusion = f32[2,8,128,128]{3,2,1,0:T(8,128)S(1)} fusion(f32[2,32,8,128]{3,2,0,1:T(8,128)S(1)} %all-to-all-done, f32[64,32]{0,1:T(8,128)S(1)} %get-tuple-element.29, f32[64,32]{0,1:T(8,128)S(1)} %get-tuple-element.30), kind=kOutput, calls=%fused_computation | convolution fusion | flops 100667392 | bytes 1327104 | tf_op jit(solution)/shard_map/kn,...nm->...km/dot_general | solution.py:34
  37.0 1.0 fusion.2
  38.3 0.6 fusion.17
  39.5 3.2 %collective-permute-start = (f32[8,4096]{1,0:T(8,128)S(1)}, f32[8,4096]{1,0:T(8,128)S(1)}, u32[]{:S(2)}, u32[]{:S(2)}) collective-permute-start(f32[8,4096]{1,0:T(8,128)S(1)} %bitcast.79), channel_id=1, source_target_pairs={{0,64},{32,0},{64,32},{1,65},{33,1},{65,33},{2,66},{34,2},{66,34},... | collective-permute-start | bytes 393224 | tf_op jit(solution)/shard_map/ppermute | solution.py:86
  42.7 3.6 %collective-permute-start.1 = (f32[8,4096]{1,0:T(8,128)S(1)}, f32[8,4096]{1,0:T(8,128)S(1)}, u32[]{:S(2)}, u32[]{:S(2)}) collective-permute-start(f32[8,4096]{1,0:T(8,128)S(1)} %bitcast.80), channel_id=1, source_target_pairs={{0,32},{32,64},{64,0},{1,33},{33,65},{65,1},{2,34},{34,66},{66,2},... | collective-permute-start | bytes 393224 | tf_op jit(solution)/shard_map/ppermute | solution.py:86
  46.3 2.3 %collective-permute-done = f32[8,4096]{1,0:T(8,128)S(1)} collective-permute-done((f32[8,4096]{1,0:T(8,128)S(1)}, f32[8,4096]{1,0:T(8,128)S(1)}, u32[]{:S(2)}, u32[]{:S(2)}) %collective-permute-start) | collective-permute-done | bytes 131104 | tf_op jit(solution)/shard_map/ppermute | solution.py:86
  48.6 2.6 %collective-permute-done.1 = f32[8,4096]{1,0:T(8,128)S(1)} collective-permute-done((f32[8,4096]{1,0:T(8,128)S(1)}, f32[8,4096]{1,0:T(8,128)S(1)}, u32[]{:S(2)}, u32[]{:S(2)}) %collective-permute-start.1) | collective-permute-done | bytes 131104 | tf_op jit(solution)/shard_map/ppermute | solution.py:86
  51.4 3.5 %collective-permute-start.2 = (f32[8,4096]{1,0:T(8,128)S(1)}, f32[8,4096]{1,0:T(8,128)S(1)}, u32[]{:S(2)}, u32[]{:S(2)}) collective-permute-start(f32[8,4096]{1,0:T(8,128)S(1)} %select_add_fusion), channel_id=1, source_target_pairs={{0,96},{96,0},{192,288},{288,192},{384,480},{480,384},{576,672},{6... | collective-permute-start | bytes 393224 | tf_op jit(solution)/shard_map/ppermute | solution.py:100
  54.9 3.8 %collective-permute-done.2 = f32[8,4096]{1,0:T(8,128)S(1)} collective-permute-done((f32[8,4096]{1,0:T(8,128)S(1)}, f32[8,4096]{1,0:T(8,128)S(1)}, u32[]{:S(2)}, u32[]{:S(2)}) %collective-permute-start.2) | collective-permute-done | bytes 131104 | tf_op jit(solution)/shard_map/ppermute | solution.py:100
  58.7 4.5 %collective-permute-start.3 = (f32[8,4096]{1,0:T(8,128)S(1)}, f32[8,4096]{1,0:T(8,128)S(1)}, u32[]{:S(2)}, u32[]{:S(2)}) collective-permute-start(f32[8,4096]{1,0:T(8,128)S(1)} %add.182), channel_id=1, source_target_pairs={{0,192},{96,288},{192,0},{288,96},{384,576},{480,672},{576,384},{6... | collective-permute-start | bytes 393224 | tf_op jit(solution)/shard_map/ppermute | solution.py:100
  63.2 1.0 fusion.6
  64.2 4.7 %collective-permute-done.3 = f32[8,4096]{1,0:T(8,128)S(1)} collective-permute-done((f32[8,4096]{1,0:T(8,128)S(1)}, f32[8,4096]{1,0:T(8,128)S(1)}, u32[]{:S(2)}, u32[]{:S(2)}) %collective-permute-start.3) | collective-permute-done | bytes 131104 | tf_op jit(solution)/shard_map/ppermute | solution.py:100
  68.9 7.7 %collective-permute-start.4 = (f32[8,4096]{1,0:T(8,128)S(1)}, f32[8,4096]{1,0:T(8,128)S(1)}, u32[]{:S(2)}, u32[]{:S(2)}) collective-permute-start(f32[8,4096]{1,0:T(8,128)S(1)} %add.183), channel_id=1, source_target_pairs={{0,384},{96,480},{192,576},{288,672},{384,0},{480,96},{576,192},{6... | collective-permute-start | bytes 393224 | tf_op jit(solution)/shard_map/ppermute | solution.py:100
  76.8 0.7 fusion
  77.5 0.9 copy.19
  78.4 4.0 %all-to-all-start.1 = ((f32[2,32,8,128]{3,2,0,1:T(8,128)}), f32[2,32,8,128]{3,2,0,1:T(8,128)S(1)}, u32[]{:S(2)}, u32[]{:S(2)}) async-start(f32[2,32,8,128]{3,2,0,1:T(8,128)} %copy.19), calls=%async_computation.1 | async-start | bytes 524288 | tf_op jit(solution)/shard_map/all_to_all | solution.py:134
  82.9 0.7 add_multiply_fusion
  83.6 17.6 %all-to-all-done.1 = f32[2,32,8,128]{3,2,0,1:T(8,128)S(1)} async-done(((f32[2,32,8,128]{3,2,0,1:T(8,128)}), f32[2,32,8,128]{3,2,0,1:T(8,128)S(1)}, u32[]{:S(2)}, u32[]{:S(2)}) %all-to-all-start.1) | async-done | bytes 262176 | tf_op jit(solution)/shard_map/all_to_all | solution.py:134
  101.2 0.8 fusion.33
  (35 shorter events, 4.1 us)
Async XLA Ops:
  0.6 18.6 %copy-start = (f32[8,4096]{1,0:T(8,128)S(1)}, f32[8,4096]{1,0:T(8,128)}, u32[]{:S(2)}) copy-start(f32[8,4096]{1,0:T(8,128)} %param.9) | copy-start | bytes 393220
  2.6 33.2 %all-to-all-start = ((f32[2,32,8,128]{3,2,0,1:T(8,128)}), f32[2,32,8,128]{3,2,0,1:T(8,128)S(1)}, u32[]{:S(2)}, u32[]{:S(2)}) async-start(f32[2,32,8,128]{3,2,0,1:T(8,128)} %copy.17), calls=%async_computation | async-start | bytes 524288 | tf_op jit(solution)/shard_map/all_to_all | solution.py:129
  39.5 9.2 %collective-permute-start = (f32[8,4096]{1,0:T(8,128)S(1)}, f32[8,4096]{1,0:T(8,128)S(1)}, u32[]{:S(2)}, u32[]{:S(2)}) collective-permute-start(f32[8,4096]{1,0:T(8,128)S(1)} %bitcast.79), channel_id=1, source_target_pairs={{0,64},{32,0},{64,32},{1,65},{33,1},{65,33},{2,66},{34,2},{66,34},... | collective-permute-start | bytes 393224 | tf_op jit(solution)/shard_map/ppermute | solution.py:86
  42.7 8.6 %collective-permute-start.1 = (f32[8,4096]{1,0:T(8,128)S(1)}, f32[8,4096]{1,0:T(8,128)S(1)}, u32[]{:S(2)}, u32[]{:S(2)}) collective-permute-start(f32[8,4096]{1,0:T(8,128)S(1)} %bitcast.80), channel_id=1, source_target_pairs={{0,32},{32,64},{64,0},{1,33},{33,65},{65,1},{2,34},{34,66},{66,2},... | collective-permute-start | bytes 393224 | tf_op jit(solution)/shard_map/ppermute | solution.py:86
  51.4 7.3 %collective-permute-start.2 = (f32[8,4096]{1,0:T(8,128)S(1)}, f32[8,4096]{1,0:T(8,128)S(1)}, u32[]{:S(2)}, u32[]{:S(2)}) collective-permute-start(f32[8,4096]{1,0:T(8,128)S(1)} %select_add_fusion), channel_id=1, source_target_pairs={{0,96},{96,0},{192,288},{288,192},{384,480},{480,384},{576,672},{6... | collective-permute-start | bytes 393224 | tf_op jit(solution)/shard_map/ppermute | solution.py:100
  58.7 10.2 %collective-permute-start.3 = (f32[8,4096]{1,0:T(8,128)S(1)}, f32[8,4096]{1,0:T(8,128)S(1)}, u32[]{:S(2)}, u32[]{:S(2)}) collective-permute-start(f32[8,4096]{1,0:T(8,128)S(1)} %add.182), channel_id=1, source_target_pairs={{0,192},{96,288},{192,0},{288,96},{384,576},{480,672},{576,384},{6... | collective-permute-start | bytes 393224 | tf_op jit(solution)/shard_map/ppermute | solution.py:100
  68.9 14.0 %collective-permute-start.4 = (f32[8,4096]{1,0:T(8,128)S(1)}, f32[8,4096]{1,0:T(8,128)S(1)}, u32[]{:S(2)}, u32[]{:S(2)}) collective-permute-start(f32[8,4096]{1,0:T(8,128)S(1)} %add.183), channel_id=1, source_target_pairs={{0,384},{96,480},{192,576},{288,672},{384,0},{480,96},{576,192},{6... | collective-permute-start | bytes 393224 | tf_op jit(solution)/shard_map/ppermute | solution.py:100
  78.4 22.8 %copy-start.4 = (f32[1,256,128]{2,1,0:T(8,128)S(1)}, f32[1,256,128]{2,1,0:T(8,128)}, u32[]{:S(2)}) copy-start(f32[1,256,128]{2,1,0:T(8,128)} %param.7) | copy-start | bytes 393220
  78.4 22.8 %all-to-all-start.1 = ((f32[2,32,8,128]{3,2,0,1:T(8,128)}), f32[2,32,8,128]{3,2,0,1:T(8,128)S(1)}, u32[]{:S(2)}, u32[]{:S(2)}) async-start(f32[2,32,8,128]{3,2,0,1:T(8,128)} %copy.19), calls=%async_computation.1 | async-start | bytes 524288 | tf_op jit(solution)/shard_map/all_to_all | solution.py:134
  82.4 18.8 %copy-start.1 = (f32[1,256,128]{2,1,0:T(8,128)S(1)}, f32[1,256,128]{2,1,0:T(8,128)}, u32[]{:S(2)}) copy-start(f32[1,256,128]{2,1,0:T(8,128)} %param.6) | copy-start | bytes 393220
  82.4 18.8 %copy-start.2 = (f32[1,256,128]{2,1,0:T(8,128)S(1)}, f32[1,256,128]{2,1,0:T(8,128)}, u32[]{:S(2)}) copy-start(f32[1,256,128]{2,1,0:T(8,128)} %param.8) | copy-start | bytes 393220
  82.4 18.8 %copy-start.3 = (f32[1,256,128]{2,1,0:T(8,128)S(1)}, f32[1,256,128]{2,1,0:T(8,128)}, u32[]{:S(2)}) copy-start(f32[1,256,128]{2,1,0:T(8,128)} %param.5) | copy-start | bytes 393220

commit v6 on v5

--- a/solution.py
+++ b/solution.py
@@ -78,21 +78,6 @@
     return (both[0], both[1], filt_local)
 
 
-def sum_in_order(part, axis):
-    size = lax.axis_size(axis)
-    me = lax.axis_index(axis)
-    held = {0: part}
-    for shift in range(1, size):
-        held[shift] = lax.ppermute(part, axis, [(j, (j + shift) % size) for j in range(size)])
-    total = None
-    for member in range(size):
-        value = held[0]
-        for shift in range(1, size):
-            value = jnp.where((me - shift) % size == member, held[shift], value)
-        total = value if total is None else total + value
-    return total
-
-
 def sum_by_doubling(part, axis):
     size = lax.axis_size(axis)
     step = 1
@@ -106,7 +91,12 @@
     if len(dp_axes) == 1:
         return lax.psum(part, dp_axes)
     wide, narrow = dp_axes
-    part = sum_in_order(part, narrow)
+    size = lax.axis_size(narrow)
+    spread = jnp.broadcast_to(part[None], (size,) + part.shape)
+    got = lax.all_to_all(spread, narrow, split_axis=0, concat_axis=0, tiled=True)
+    part = got[0]
+    for member in range(1, size):
+        part = part + got[member]
     return sum_by_doubling(part, wide)
 
 

time: 103 us -> 91.3 us (0.89)
  the two profiles are of different devices: /device:TPU:128 before, /device:TPU:1 now
where the time goes in v6:
time: 91.3 us; the launch traced here: 90.9 us
  starting transfers between devices  44.8 us (49%)
  waiting for transfers between devices  31.5 us (35%)
  matrix products  6.03 us (7%)
  other arithmetic  5.01 us (5%)
  local copies, waits for them, and re-layouts  2.6 us (3%)
  between operations  0.96 us (1%)
    all_to_all x1, starting transfers between devices, body_steps(): got = lax.all_to_all(sent, 'seq', split_axis=1, concat_axis=1, tiled=True)  18.6 us
    ppermute x3, starting transfers between devices, sum_by_doubling(): part = part + lax.ppermute(part, axis, [(j, j ^ step) for j in range(size)])  13.6 us
    ppermute x3, waiting for transfers between devices, sum_by_doubling(): part = part + lax.ppermute(part, axis, [(j, j ^ step) for j in range(size)])  13 us
    all_to_all x1, waiting for transfers between devices, body_steps(): got = lax.all_to_all(sent, 'seq', split_axis=1, concat_axis=1, tiled=True)  11.1 us
    all_to_all x1, starting transfers between devices, reduce_filter(): lax.all_to_all(spread, narrow, split_axis=0, concat_axis=0, tiled=True)  7.43 us
    all_to_all x1, waiting for transfers between devices, reduce_filter(): lax.all_to_all(spread, narrow, split_axis=0, concat_axis=0, tiled=True)  7.36 us
    all_to_all x1, starting transfers between devices, body_steps(): back = lax.all_to_all(back, 'seq', split_axis=1, concat_axis=1, tiled=True)  5.17 us
  transfers between devices with their start and end apart: 6, of which 4 were waited for; matrix products, arithmetic and copies ran while one was open for 7% of the time, Pallas kernels for 0%

profile of v6, /device:TPU:1, one launch (start us, length us, event | category | flops | bytes accessed | tf_op | source)
XLA Modules:
  0.0 90.9 jit_solution(6299215655274877949)
XLA Ops:
  0.6 1.2 %multiply_bitcast_fusion = (f32[1,32,8,128]{3,2,1,0:T(8,128)S(1)}, f32[1,32,8,128]{3,2,1,0:T(8,128)S(1)}) fusion(f32[1,256,128]{2,1,0:T(8,128)} %param.8, f32[1,256,128]{2,1,0:T(8,128)} %param.5, f32[1,256,128]{2,1,0:T(8,128)} %param.6, f32[1,256,128]{2,1,0:T(8,128)} %param.7), kind=kLoop, calls=%fused_computation.63 | loop fusion | flops 65536 | bytes 786432 | tf_op jit(solution)/shard_map/stack | solution.py:118
  1.8 0.7 copy.17
  2.6 18.6 %all-to-all-start = ((f32[2,32,8,128]{3,2,0,1:T(8,128)}), f32[2,32,8,128]{3,2,0,1:T(8,128)S(1)}, u32[]{:S(2)}, u32[]{:S(2)}) async-start(f32[2,32,8,128]{3,2,0,1:T(8,128)} %copy.17), calls=%async_computation | async-start | bytes 524288 | tf_op jit(solution)/shard_map/all_to_all | solution.py:119
  22.8 0.7 convolution_bitcast_fusion.1
  23.5 0.6 fusion.13
  24.1 11.1 %all-to-all-done = f32[2,32,8,128]{3,2,0,1:T(8,128)S(1)} async-done(((f32[2,32,8,128]{3,2,0,1:T(8,128)}), f32[2,32,8,128]{3,2,0,1:T(8,128)S(1)}, u32[]{:S(2)}, u32[]{:S(2)}) %all-to-all-start) | async-done | bytes 262176 | tf_op jit(solution)/shard_map/all_to_all | solution.py:119
  35.3 1.1 %convolution_bitcast_fusion = f32[2,8,128,128]{3,2,1,0:T(8,128)S(1)} fusion(f32[2,32,8,128]{3,2,0,1:T(8,128)S(1)} %all-to-all-done, f32[64,32]{0,1:T(8,128)S(1)} %get-tuple-element.29, f32[64,32]{0,1:T(8,128)S(1)} %get-tuple-element.30), kind=kOutput, calls=%fused_computation | convolution fusion | flops 100667392 | bytes 1327104 | tf_op jit(solution)/shard_map/kn,...nm->...km/dot_general | solution.py:34
  36.5 1.0 %fusion.2 = f32[2,8,64,256]{3,2,1,0:T(8,128)S(1)} fusion(f32[2,8,64,128]{3,2,1,0:T(8,128)S(1)} %get-tuple-element.8, f32[2,8,64,128]{3,2,1,0:T(8,128)S(1)} %get-tuple-element.7, f32[128,128]{1,0:T(8,128)S(1)} %get-tuple-element.34, f32[128,128]{1,0:T(8,128)S(1)} %fusion.46, f32[128,128]{1,0:T(8,128)S(1)} %get-tuple-element.33), kind=kOutput, calls=%fused_computation.6 | convolution fusion | flops 805765120 | bytes 2293760 | tf_op jit(solution)/shard_map/...n,nk->...k/dot_general | solution.py:41
  37.8 0.6 fusion.17
  38.5 0.4 fusion.1
  39.0 0.8 broadcast_in_dim.2
  39.8 7.4 %all-to-all-start.2 = ((f32[3,8,4096]{2,1,0:T(8,128)}), f32[3,8,4096]{2,1,0:T(8,128)S(1)}, u32[]{:S(2)}, u32[]{:S(2)}) async-start(f32[3,8,4096]{2,1,0:T(8,128)} %broadcast_in_dim.2), calls=%async_computation.2 | async-start | bytes 786432 | tf_op jit(solution)/shard_map/all_to_all | solution.py:96
  47.4 1.0 %fusion.6 = f32[2,8,64,256]{3,2,1,0:T(8,128)S(1)} fusion(f32[1,8,64,256]{3,2,1,0:T(8,128)S(1)} %maximum_bitcast_fusion.1, f32[1,8,64,256]{3,2,1,0:T(8,128)S(1)} %maximum_bitcast_fusion, f32[128,128]{1,0:T(8,128)S(1)} %get-tuple-element.36, f32[128,128]{1,0:T(8,128)S(1)} %fusion.47, f32[128,128]{1,0:T(8,128)S(1)} %get-tuple-element.35), kind=kOutput, calls=%fused_computation.10 | convolution fusion | flops 805765120 | bytes 2293760 | tf_op jit(solution)/shard_map/...n,nk->...k/dot_general | solution.py:46
  48.4 7.4 %all-to-all-done.2 = f32[3,8,4096]{2,1,0:T(8,128)S(1)} async-done(((f32[3,8,4096]{2,1,0:T(8,128)}), f32[3,8,4096]{2,1,0:T(8,128)S(1)}, u32[]{:S(2)}, u32[]{:S(2)}) %all-to-all-start.2) | async-done | bytes 393248 | tf_op jit(solution)/shard_map/all_to_all | solution.py:96
  55.7 3.2 %collective-permute-start = (f32[8,4096]{1,0:T(8,128)S(1)}, f32[8,4096]{1,0:T(8,128)S(1)}, u32[]{:S(2)}, u32[]{:S(2)}) collective-permute-start(f32[8,4096]{1,0:T(8,128)S(1)} %fusion.30), channel_id=1, source_target_pairs={{0,96},{96,0},{192,288},{288,192},{384,480},{480,384},{576,672},{6... | collective-permute-start | bytes 393224 | tf_op jit(solution)/shard_map/ppermute | solution.py:85
  59.1 0.7 fusion
  59.8 0.9 copy.19
  60.7 5.2 %all-to-all-start.1 = ((f32[2,32,8,128]{3,2,0,1:T(8,128)}), f32[2,32,8,128]{3,2,0,1:T(8,128)S(1)}, u32[]{:S(2)}, u32[]{:S(2)}) async-start(f32[2,32,8,128]{3,2,0,1:T(8,128)} %copy.19), calls=%async_computation.1 | async-start | bytes 524288 | tf_op jit(solution)/shard_map/all_to_all | solution.py:124
  65.9 4.3 %collective-permute-start.1 = (f32[8,4096]{1,0:T(8,128)S(1)}, f32[8,4096]{1,0:T(8,128)S(1)}, u32[]{:S(2)}, u32[]{:S(2)}) collective-permute-start(f32[8,4096]{1,0:T(8,128)S(1)} %fusion.75), channel_id=1, source_target_pairs={{0,192},{96,288},{192,0},{288,96},{384,576},{480,672},{576,384},{6... | collective-permute-start | bytes 393224 | tf_op jit(solution)/shard_map/ppermute | solution.py:85
  70.3 6.7 %collective-permute-done.1 = f32[8,4096]{1,0:T(8,128)S(1)} collective-permute-done((f32[8,4096]{1,0:T(8,128)S(1)}, f32[8,4096]{1,0:T(8,128)S(1)}, u32[]{:S(2)}, u32[]{:S(2)}) %collective-permute-start.1) | collective-permute-done | bytes 131104 | tf_op jit(solution)/shard_map/ppermute | solution.py:85
  77.0 6.0 %collective-permute-start.2 = (f32[8,4096]{1,0:T(8,128)S(1)}, f32[8,4096]{1,0:T(8,128)S(1)}, u32[]{:S(2)}, u32[]{:S(2)}) collective-permute-start(f32[8,4096]{1,0:T(8,128)S(1)} %add.173), channel_id=1, source_target_pairs={{0,384},{96,480},{192,576},{288,672},{384,0},{480,96},{576,192},{6... | collective-permute-start | bytes 393224 | tf_op jit(solution)/shard_map/ppermute | solution.py:85
  83.1 0.8 fusion.34
  83.9 6.3 %collective-permute-done.2 = f32[8,4096]{1,0:T(8,128)S(1)} collective-permute-done((f32[8,4096]{1,0:T(8,128)S(1)}, f32[8,4096]{1,0:T(8,128)S(1)}, u32[]{:S(2)}, u32[]{:S(2)}) %collective-permute-start.2) | collective-permute-done | bytes 131104 | tf_op jit(solution)/shard_map/ppermute | solution.py:85
  90.2 0.7 add_multiply_fusion
  (34 shorter events, 2.6 us)
Async XLA Ops:
  0.6 22.1 %copy-start = (f32[8,4096]{1,0:T(8,128)S(1)}, f32[8,4096]{1,0:T(8,128)}, u32[]{:S(2)}) copy-start(f32[8,4096]{1,0:T(8,128)} %param.9) | copy-start | bytes 393220
  2.6 32.7 %all-to-all-start = ((f32[2,32,8,128]{3,2,0,1:T(8,128)}), f32[2,32,8,128]{3,2,0,1:T(8,128)S(1)}, u32[]{:S(2)}, u32[]{:S(2)}) async-start(f32[2,32,8,128]{3,2,0,1:T(8,128)} %copy.17), calls=%async_computation | async-start | bytes 524288 | tf_op jit(solution)/shard_map/all_to_all | solution.py:119
  39.8 15.9 %all-to-all-start.2 = ((f32[3,8,4096]{2,1,0:T(8,128)}), f32[3,8,4096]{2,1,0:T(8,128)S(1)}, u32[]{:S(2)}, u32[]{:S(2)}) async-start(f32[3,8,4096]{2,1,0:T(8,128)} %broadcast_in_dim.2), calls=%async_computation.2 | async-start | bytes 786432 | tf_op jit(solution)/shard_map/all_to_all | solution.py:96
  55.7 10.1 %collective-permute-start = (f32[8,4096]{1,0:T(8,128)S(1)}, f32[8,4096]{1,0:T(8,128)S(1)}, u32[]{:S(2)}, u32[]{:S(2)}) collective-permute-start(f32[8,4096]{1,0:T(8,128)S(1)} %fusion.30), channel_id=1, source_target_pairs={{0,96},{96,0},{192,288},{288,192},{384,480},{480,384},{576,672},{6... | collective-permute-start | bytes 393224 | tf_op jit(solution)/shard_map/ppermute | solution.py:85
  60.7 22.4 %all-to-all-start.1 = ((f32[2,32,8,128]{3,2,0,1:T(8,128)}), f32[2,32,8,128]{3,2,0,1:T(8,128)S(1)}, u32[]{:S(2)}, u32[]{:S(2)}) async-start(f32[2,32,8,128]{3,2,0,1:T(8,128)} %copy.19), calls=%async_computation.1 | async-start | bytes 524288 | tf_op jit(solution)/shard_map/all_to_all | solution.py:124
  65.9 17.2 %copy-start.4 = (f32[1,256,128]{2,1,0:T(8,128)S(1)}, f32[1,256,128]{2,1,0:T(8,128)}, u32[]{:S(2)}) copy-start(f32[1,256,128]{2,1,0:T(8,128)} %param.7) | copy-start | bytes 393220
  65.9 17.2 %copy-start.1 = (f32[1,256,128]{2,1,0:T(8,128)S(1)}, f32[1,256,128]{2,1,0:T(8,128)}, u32[]{:S(2)}) copy-start(f32[1,256,128]{2,1,0:T(8,128)} %param.6) | copy-start | bytes 393220
  65.9 17.2 %copy-start.2 = (f32[1,256,128]{2,1,0:T(8,128)S(1)}, f32[1,256,128]{2,1,0:T(8,128)}, u32[]{:S(2)}) copy-start(f32[1,256,128]{2,1,0:T(8,128)} %param.8) | copy-start | bytes 393220
  65.9 17.2 %copy-start.3 = (f32[1,256,128]{2,1,0:T(8,128)S(1)}, f32[1,256,128]{2,1,0:T(8,128)}, u32[]{:S(2)}) copy-start(f32[1,256,128]{2,1,0:T(8,128)} %param.5) | copy-start | bytes 393220
  65.9 11.1 %collective-permute-start.1 = (f32[8,4096]{1,0:T(8,128)S(1)}, f32[8,4096]{1,0:T(8,128)S(1)}, u32[]{:S(2)}, u32[]{:S(2)}) collective-permute-start(f32[8,4096]{1,0:T(8,128)S(1)} %fusion.75), channel_id=1, source_target_pairs={{0,192},{96,288},{192,0},{288,96},{384,576},{480,672},{576,384},{6... | collective-permute-start | bytes 393224 | tf_op jit(solution)/shard_map/ppermute | solution.py:85
  77.0 13.2 %collective-permute-start.2 = (f32[8,4096]{1,0:T(8,128)S(1)}, f32[8,4096]{1,0:T(8,128)S(1)}, u32[]{:S(2)}, u32[]{:S(2)}) collective-permute-start(f32[8,4096]{1,0:T(8,128)S(1)} %add.173), channel_id=1, source_target_pairs={{0,384},{96,480},{192,576},{288,672},{384,0},{480,96},{576,192},{6... | collective-permute-start | bytes 393224 | tf_op jit(solution)/shard_map/ppermute | solution.py:85

commit v7 on v5

--- a/solution.py
+++ b/solution.py
@@ -82,7 +82,7 @@
     size = lax.axis_size(axis)
     me = lax.axis_index(axis)
     held = {0: part}
-    for shift in range(1, size):
+    for shift in range(size - 1, 0, -1):
         held[shift] = lax.ppermute(part, axis, [(j, (j + shift) % size) for j in range(size)])
     total = None
     for member in range(size):
@@ -95,10 +95,10 @@
 
 def sum_by_doubling(part, axis):
     size = lax.axis_size(axis)
-    step = 1
-    while step < size:
+    step = size // 2
+    while step >= 1:
         part = part + lax.ppermute(part, axis, [(j, j ^ step) for j in range(size)])
-        step *= 2
+        step //= 2
     return part
 
 

time: 103 us -> 105 us (1.019)
  the two profiles are of different devices: /device:TPU:128 before, /device:TPU:41 now
where the time goes in v7:
time: 105 us; the launch traced here: 104 us
  starting transfers between devices  49.2 us (47%)
  waiting for transfers between devices  41.1 us (39%)
  matrix products  6.05 us (6%)
  other arithmetic  5.08 us (5%)
  local copies, waits for them, and re-layouts  1.81 us (2%)
    all_to_all x1, starting transfers between devices, body_steps(): got = lax.all_to_all(sent, 'seq', split_axis=1, concat_axis=1, tiled=True)  17.8 us
    all_to_all x1, waiting for transfers between devices, body_steps(): back = lax.all_to_all(back, 'seq', split_axis=1, concat_axis=1, tiled=True)  14.9 us
    all_to_all x1, waiting for transfers between devices, body_steps(): got = lax.all_to_all(sent, 'seq', split_axis=1, concat_axis=1, tiled=True)  11.1 us
    all_to_all x1, starting transfers between devices, body_steps(): back = lax.all_to_all(back, 'seq', split_axis=1, concat_axis=1, tiled=True)  10.7 us
    ppermute x3, starting transfers between devices, sum_by_doubling(): part = part + lax.ppermute(part, axis, [(j, j ^ step) for j in range(size)])  10.7 us
    ppermute x2, starting transfers between devices, sum_in_order(): lax.ppermute(part, axis, [(j, (j + shift) % size) for j in range(size)])  9.98 us
    ppermute x3, waiting for transfers between devices, sum_by_doubling(): part = part + lax.ppermute(part, axis, [(j, j ^ step) for j in range(size)])  9.33 us
    ppermute x2, waiting for transfers between devices, sum_in_order(): lax.ppermute(part, axis, [(j, (j + shift) % size) for j in range(size)])  5.82 us
  transfers between devices with their start and end apart: 7, of which 6 were waited for; matrix products, arithmetic and copies ran while one was open for 6% of the time, Pallas kernels for 0%

profile of v7, /device:TPU:41, one launch (start us, length us, event | category | flops | bytes accessed | tf_op | source)
XLA Modules:
  0.0 104.3 jit_solution(6015171490938390662)
XLA Ops:
  0.6 1.2 %multiply_bitcast_fusion = (f32[1,32,8,128]{3,2,1,0:T(8,128)S(1)}, f32[1,32,8,128]{3,2,1,0:T(8,128)S(1)}) fusion(f32[1,256,128]{2,1,0:T(8,128)} %param.8, f32[1,256,128]{2,1,0:T(8,128)} %param.5, f32[1,256,128]{2,1,0:T(8,128)} %param.6, f32[1,256,128]{2,1,0:T(8,128)} %param.7), kind=kLoop, calls=%fused_computation.61 | loop fusion | flops 65536 | bytes 786432 | tf_op jit(solution)/shard_map/stack | solution.py:128
  1.8 0.7 copy.17
  2.6 17.8 %all-to-all-start = ((f32[2,32,8,128]{3,2,0,1:T(8,128)}), f32[2,32,8,128]{3,2,0,1:T(8,128)S(1)}, u32[]{:S(2)}, u32[]{:S(2)}) async-start(f32[2,32,8,128]{3,2,0,1:T(8,128)} %copy.17), calls=%async_computation | async-start | bytes 524288 | tf_op jit(solution)/shard_map/all_to_all | solution.py:129
  22.0 0.7 convolution_bitcast_fusion.1
  22.8 0.6 fusion.13
  23.4 11.1 %all-to-all-done = f32[2,32,8,128]{3,2,0,1:T(8,128)S(1)} async-done(((f32[2,32,8,128]{3,2,0,1:T(8,128)}), f32[2,32,8,128]{3,2,0,1:T(8,128)S(1)}, u32[]{:S(2)}, u32[]{:S(2)}) %all-to-all-start) | async-done | bytes 262176 | tf_op jit(solution)/shard_map/all_to_all | solution.py:129
  34.5 1.1 %convolution_bitcast_fusion = f32[2,8,128,128]{3,2,1,0:T(8,128)S(1)} fusion(f32[2,32,8,128]{3,2,0,1:T(8,128)S(1)} %all-to-all-done, f32[64,32]{0,1:T(8,128)S(1)} %get-tuple-element.29, f32[64,32]{0,1:T(8,128)S(1)} %get-tuple-element.30), kind=kOutput, calls=%fused_computation | convolution fusion | flops 100667392 | bytes 1327104 | tf_op jit(solution)/shard_map/kn,...nm->...km/dot_general | solution.py:34
  35.7 1.0 fusion.2
  38.2 8.1 %collective-permute-start = (f32[8,4096]{1,0:T(8,128)S(1)}, f32[8,4096]{1,0:T(8,128)S(1)}, u32[]{:S(2)}, u32[]{:S(2)}) collective-permute-start(f32[8,4096]{1,0:T(8,128)S(1)} %bitcast.79), channel_id=1, source_target_pairs={{0,64},{32,0},{64,32},{1,65},{33,1},{65,33},{2,66},{34,2},{66,34},... | collective-permute-start | bytes 393224 | tf_op jit(solution)/shard_map/ppermute | solution.py:86
  46.2 1.9 %collective-permute-start.1 = (f32[8,4096]{1,0:T(8,128)S(1)}, f32[8,4096]{1,0:T(8,128)S(1)}, u32[]{:S(2)}, u32[]{:S(2)}) collective-permute-start(f32[8,4096]{1,0:T(8,128)S(1)} %bitcast.80), channel_id=1, source_target_pairs={{0,32},{32,64},{64,0},{1,33},{33,65},{65,1},{2,34},{34,66},{66,2},... | collective-permute-start | bytes 393224 | tf_op jit(solution)/shard_map/ppermute | solution.py:86
  48.3 1.3 %collective-permute-done = f32[8,4096]{1,0:T(8,128)S(1)} collective-permute-done((f32[8,4096]{1,0:T(8,128)S(1)}, f32[8,4096]{1,0:T(8,128)S(1)}, u32[]{:S(2)}, u32[]{:S(2)}) %collective-permute-start) | collective-permute-done | bytes 131104 | tf_op jit(solution)/shard_map/ppermute | solution.py:86
  49.6 4.5 %collective-permute-done.1 = f32[8,4096]{1,0:T(8,128)S(1)} collective-permute-done((f32[8,4096]{1,0:T(8,128)S(1)}, f32[8,4096]{1,0:T(8,128)S(1)}, u32[]{:S(2)}, u32[]{:S(2)}) %collective-permute-start.1) | collective-permute-done | bytes 131104 | tf_op jit(solution)/shard_map/ppermute | solution.py:86
  54.2 2.6 %collective-permute-start.2 = (f32[8,4096]{1,0:T(8,128)S(1)}, f32[8,4096]{1,0:T(8,128)S(1)}, u32[]{:S(2)}, u32[]{:S(2)}) collective-permute-start(f32[8,4096]{1,0:T(8,128)S(1)} %select_add_fusion), channel_id=1, source_target_pairs={{0,384},{96,480},{192,576},{288,672},{384,0},{480,96},{576,192},{6... | collective-permute-start | bytes 393224 | tf_op jit(solution)/shard_map/ppermute | solution.py:100
  56.9 7.9 %collective-permute-done.2 = f32[8,4096]{1,0:T(8,128)S(1)} collective-permute-done((f32[8,4096]{1,0:T(8,128)S(1)}, f32[8,4096]{1,0:T(8,128)S(1)}, u32[]{:S(2)}, u32[]{:S(2)}) %collective-permute-start.2) | collective-permute-done | bytes 131104 | tf_op jit(solution)/shard_map/ppermute | solution.py:100
  64.8 4.9 %collective-permute-start.3 = (f32[8,4096]{1,0:T(8,128)S(1)}, f32[8,4096]{1,0:T(8,128)S(1)}, u32[]{:S(2)}, u32[]{:S(2)}) collective-permute-start(f32[8,4096]{1,0:T(8,128)S(1)} %add.182), channel_id=1, source_target_pairs={{0,192},{96,288},{192,0},{288,96},{384,576},{480,672},{576,384},{6... | collective-permute-start | bytes 393224 | tf_op jit(solution)/shard_map/ppermute | solution.py:100
  69.8 1.0 fusion.6
  70.8 1.4 %collective-permute-done.3 = f32[8,4096]{1,0:T(8,128)S(1)} collective-permute-done((f32[8,4096]{1,0:T(8,128)S(1)}, f32[8,4096]{1,0:T(8,128)S(1)}, u32[]{:S(2)}, u32[]{:S(2)}) %collective-permute-start.3) | collective-permute-done | bytes 131104 | tf_op jit(solution)/shard_map/ppermute | solution.py:100
  72.2 3.1 %collective-permute-start.4 = (f32[8,4096]{1,0:T(8,128)S(1)}, f32[8,4096]{1,0:T(8,128)S(1)}, u32[]{:S(2)}, u32[]{:S(2)}) collective-permute-start(f32[8,4096]{1,0:T(8,128)S(1)} %add.183), channel_id=1, source_target_pairs={{0,96},{96,0},{192,288},{288,192},{384,480},{480,384},{576,672},{6... | collective-permute-start | bytes 393224 | tf_op jit(solution)/shard_map/ppermute | solution.py:100
  75.5 0.7 fusion
  76.2 0.9 copy.19
  77.1 10.7 %all-to-all-start.1 = ((f32[2,32,8,128]{3,2,0,1:T(8,128)}), f32[2,32,8,128]{3,2,0,1:T(8,128)S(1)}, u32[]{:S(2)}, u32[]{:S(2)}) async-start(f32[2,32,8,128]{3,2,0,1:T(8,128)} %copy.19), calls=%async_computation.1 | async-start | bytes 524288 | tf_op jit(solution)/shard_map/all_to_all | solution.py:134
  87.9 0.7 add_multiply_fusion
  88.5 14.9 %all-to-all-done.1 = f32[2,32,8,128]{3,2,0,1:T(8,128)S(1)} async-done(((f32[2,32,8,128]{3,2,0,1:T(8,128)}), f32[2,32,8,128]{3,2,0,1:T(8,128)S(1)}, u32[]{:S(2)}, u32[]{:S(2)}) %all-to-all-start.1) | async-done | bytes 262176 | tf_op jit(solution)/shard_map/all_to_all | solution.py:134
  103.5 0.8 fusion.33
  (35 shorter events, 3.7 us)
Async XLA Ops:
  0.6 21.4 %copy-start = (f32[8,4096]{1,0:T(8,128)S(1)}, f32[8,4096]{1,0:T(8,128)}, u32[]{:S(2)}) copy-start(f32[8,4096]{1,0:T(8,128)} %param.9) | copy-start | bytes 393220
  2.6 31.9 %all-to-all-start = ((f32[2,32,8,128]{3,2,0,1:T(8,128)}), f32[2,32,8,128]{3,2,0,1:T(8,128)S(1)}, u32[]{:S(2)}, u32[]{:S(2)}) async-start(f32[2,32,8,128]{3,2,0,1:T(8,128)} %copy.17), calls=%async_computation | async-start | bytes 524288 | tf_op jit(solution)/shard_map/all_to_all | solution.py:129
  38.2 11.4 %collective-permute-start = (f32[8,4096]{1,0:T(8,128)S(1)}, f32[8,4096]{1,0:T(8,128)S(1)}, u32[]{:S(2)}, u32[]{:S(2)}) collective-permute-start(f32[8,4096]{1,0:T(8,128)S(1)} %bitcast.79), channel_id=1, source_target_pairs={{0,64},{32,0},{64,32},{1,65},{33,1},{65,33},{2,66},{34,2},{66,34},... | collective-permute-start | bytes 393224 | tf_op jit(solution)/shard_map/ppermute | solution.py:86
  46.2 7.8 %collective-permute-start.1 = (f32[8,4096]{1,0:T(8,128)S(1)}, f32[8,4096]{1,0:T(8,128)S(1)}, u32[]{:S(2)}, u32[]{:S(2)}) collective-permute-start(f32[8,4096]{1,0:T(8,128)S(1)} %bitcast.80), channel_id=1, source_target_pairs={{0,32},{32,64},{64,0},{1,33},{33,65},{65,1},{2,34},{34,66},{66,2},... | collective-permute-start | bytes 393224 | tf_op jit(solution)/shard_map/ppermute | solution.py:86
  54.2 10.6 %collective-permute-start.2 = (f32[8,4096]{1,0:T(8,128)S(1)}, f32[8,4096]{1,0:T(8,128)S(1)}, u32[]{:S(2)}, u32[]{:S(2)}) collective-permute-start(f32[8,4096]{1,0:T(8,128)S(1)} %select_add_fusion), channel_id=1, source_target_pairs={{0,384},{96,480},{192,576},{288,672},{384,0},{480,96},{576,192},{6... | collective-permute-start | bytes 393224 | tf_op jit(solution)/shard_map/ppermute | solution.py:100
  64.8 7.4 %collective-permute-start.3 = (f32[8,4096]{1,0:T(8,128)S(1)}, f32[8,4096]{1,0:T(8,128)S(1)}, u32[]{:S(2)}, u32[]{:S(2)}) collective-permute-start(f32[8,4096]{1,0:T(8,128)S(1)} %add.182), channel_id=1, source_target_pairs={{0,192},{96,288},{192,0},{288,96},{384,576},{480,672},{576,384},{6... | collective-permute-start | bytes 393224 | tf_op jit(solution)/shard_map/ppermute | solution.py:100
  72.2 15.6 %collective-permute-start.4 = (f32[8,4096]{1,0:T(8,128)S(1)}, f32[8,4096]{1,0:T(8,128)S(1)}, u32[]{:S(2)}, u32[]{:S(2)}) collective-permute-start(f32[8,4096]{1,0:T(8,128)S(1)} %add.183), channel_id=1, source_target_pairs={{0,96},{96,0},{192,288},{288,192},{384,480},{480,384},{576,672},{6... | collective-permute-start | bytes 393224 | tf_op jit(solution)/shard_map/ppermute | solution.py:100
  77.1 26.3 %copy-start.4 = (f32[1,256,128]{2,1,0:T(8,128)S(1)}, f32[1,256,128]{2,1,0:T(8,128)}, u32[]{:S(2)}) copy-start(f32[1,256,128]{2,1,0:T(8,128)} %param.7) | copy-start | bytes 393220
  77.1 26.3 %all-to-all-start.1 = ((f32[2,32,8,128]{3,2,0,1:T(8,128)}), f32[2,32,8,128]{3,2,0,1:T(8,128)S(1)}, u32[]{:S(2)}, u32[]{:S(2)}) async-start(f32[2,32,8,128]{3,2,0,1:T(8,128)} %copy.19), calls=%async_computation.1 | async-start | bytes 524288 | tf_op jit(solution)/shard_map/all_to_all | solution.py:134
  87.8 15.6 %copy-start.1 = (f32[1,256,128]{2,1,0:T(8,128)S(1)}, f32[1,256,128]{2,1,0:T(8,128)}, u32[]{:S(2)}) copy-start(f32[1,256,128]{2,1,0:T(8,128)} %param.6) | copy-start | bytes 393220
  87.8 15.6 %copy-start.2 = (f32[1,256,128]{2,1,0:T(8,128)S(1)}, f32[1,256,128]{2,1,0:T(8,128)}, u32[]{:S(2)}) copy-start(f32[1,256,128]{2,1,0:T(8,128)} %param.8) | copy-start | bytes 393220
  87.8 15.6 %copy-start.3 = (f32[1,256,128]{2,1,0:T(8,128)S(1)}, f32[1,256,128]{2,1,0:T(8,128)}, u32[]{:S(2)}) copy-start(f32[1,256,128]{2,1,0:T(8,128)} %param.5) | copy-start | bytes 393220

commit v8 on v7

--- a/solution.py
+++ b/solution.py
@@ -82,7 +82,7 @@
     size = lax.axis_size(axis)
     me = lax.axis_index(axis)
     held = {0: part}
-    for shift in range(size - 1, 0, -1):
+    for shift in range(1, size):
         held[shift] = lax.ppermute(part, axis, [(j, (j + shift) % size) for j in range(size)])
     total = None
     for member in range(size):
@@ -123,9 +123,7 @@
     channels = query.shape[1]
     local = query.shape[2]
     per = channels // parts
-    gated = key_in[0] * value[0]
-    grad_conv = grad_out[0] * query[0]
-    sent = jnp.stack([gated, grad_conv]).reshape(2, parts, per, local)
+    sent = (jnp.stack([key_in[0], grad_out[0]]) * jnp.stack([value[0], query[0]])).reshape(2, parts, per, local)
     got = lax.all_to_all(sent, "seq", split_axis=1, concat_axis=1, tiled=True)
     got = jnp.swapaxes(got, 1, 2).reshape(2, per, length)
     conv, grad_gated, filt_local = convolve_all(got[0], got[1], filt)

time: 105 us -> 105 us (level)
    another operation x2 -> x0, other arithmetic: 1.18 us -> none  [body_steps(): sent = jnp.stack([gated, grad_conv]).reshape(2, parts, per, local)]
    mul x0 -> x1, other arithmetic: none -> 1.16 us  [body_steps(): jnp.stack([key_in[0], grad_out[0]]) * jnp.stack([value[0], query[0]])]
where the time goes in v8:
time: 105 us; the launch traced here: 104 us
  starting transfers between devices  49.2 us (47%)
  waiting for transfers between devices  41.1 us (39%)
  matrix products  6.04 us (6%)
  other arithmetic  5.06 us (5%)
  local copies, waits for them, and re-layouts  1.77 us (2%)
    all_to_all x1, starting transfers between devices, body_steps(): got = lax.all_to_all(sent, 'seq', split_axis=1, concat_axis=1, tiled=True)  17.8 us
    all_to_all x1, waiting for transfers between devices, body_steps(): back = lax.all_to_all(back, 'seq', split_axis=1, concat_axis=1, tiled=True)  14.9 us
    all_to_all x1, waiting for transfers between devices, body_steps(): got = lax.all_to_all(sent, 'seq', split_axis=1, concat_axis=1, tiled=True)  11.1 us
    all_to_all x1, starting transfers between devices, body_steps(): back = lax.all_to_all(back, 'seq', split_axis=1, concat_axis=1, tiled=True)  10.7 us
    ppermute x3, starting transfers between devices, sum_by_doubling(): part = part + lax.ppermute(part, axis, [(j, j ^ step) for j in range(size)])  10.7 us
    ppermute x2, starting transfers between devices, sum_in_order(): lax.ppermute(part, axis, [(j, (j + shift) % size) for j in range(size)])  9.98 us
    ppermute x3, waiting for transfers between devices, sum_by_doubling(): part = part + lax.ppermute(part, axis, [(j, j ^ step) for j in range(size)])  9.35 us
    ppermute x2, waiting for transfers between devices, sum_in_order(): lax.ppermute(part, axis, [(j, (j + shift) % size) for j in range(size)])  5.83 us
  transfers between devices with their start and end apart: 7, of which 6 were waited for; matrix products, arithmetic and copies ran while one was open for 6% of the time, Pallas kernels for 0%

profile of v8, /device:TPU:41, one launch (start us, length us, event | category | flops | bytes accessed | tf_op | source)
XLA Modules:
  0.0 104.1 jit_solution(10087365074479305943)
XLA Ops:
  0.6 1.2 %maximum_multiply_fusion = f32[2,32,8,128]{3,2,1,0:T(8,128)S(1)} fusion(f32[1,32,8,128]{3,2,1,0:T(8,128)} %bitcast.80, f32[1,32,8,128]{3,2,1,0:T(8,128)} %bitcast.79, f32[1,32,8,128]{3,2,1,0:T(8,128)} %bitcast.81, f32[1,32,8,128]{3,2,1,0:T(8,128)} %bitcast.82), kind=kLoop, calls=%fused_computation.37 | loop fusion | flops 196608 | bytes 786432 | tf_op jit(solution)/shard_map/mul | solution.py:126
  1.8 0.7 copy.19
  2.5 17.8 %all-to-all-start = ((f32[2,32,8,128]{3,2,0,1:T(8,128)}), f32[2,32,8,128]{3,2,0,1:T(8,128)S(1)}, u32[]{:S(2)}, u32[]{:S(2)}) async-start(f32[2,32,8,128]{3,2,0,1:T(8,128)} %copy.19), calls=%async_computation | async-start | bytes 524288 | tf_op jit(solution)/shard_map/all_to_all | solution.py:127
  22.0 0.7 convolution_bitcast_fusion.1
  22.7 0.6 fusion.13
  23.3 11.1 %all-to-all-done = f32[2,32,8,128]{3,2,0,1:T(8,128)S(1)} async-done(((f32[2,32,8,128]{3,2,0,1:T(8,128)}), f32[2,32,8,128]{3,2,0,1:T(8,128)S(1)}, u32[]{:S(2)}, u32[]{:S(2)}) %all-to-all-start) | async-done | bytes 262176 | tf_op jit(solution)/shard_map/all_to_all | solution.py:127
  34.4 1.1 %convolution_bitcast_fusion = f32[2,8,128,128]{3,2,1,0:T(8,128)S(1)} fusion(f32[2,32,8,128]{3,2,0,1:T(8,128)S(1)} %all-to-all-done, f32[64,32]{0,1:T(8,128)S(1)} %get-tuple-element.27, f32[64,32]{0,1:T(8,128)S(1)} %get-tuple-element.28), kind=kOutput, calls=%fused_computation | convolution fusion | flops 100667392 | bytes 1327104 | tf_op jit(solution)/shard_map/kn,...nm->...km/dot_general | solution.py:34
  35.7 1.0 fusion.2
  38.1 8.1 %collective-permute-start = (f32[8,4096]{1,0:T(8,128)S(1)}, f32[8,4096]{1,0:T(8,128)S(1)}, u32[]{:S(2)}, u32[]{:S(2)}) collective-permute-start(f32[8,4096]{1,0:T(8,128)S(1)} %bitcast.83), channel_id=1, source_target_pairs={{0,64},{32,0},{64,32},{1,65},{33,1},{65,33},{2,66},{34,2},{66,34},... | collective-permute-start | bytes 393224 | tf_op jit(solution)/shard_map/ppermute | solution.py:86
  46.2 1.9 %collective-permute-start.1 = (f32[8,4096]{1,0:T(8,128)S(1)}, f32[8,4096]{1,0:T(8,128)S(1)}, u32[]{:S(2)}, u32[]{:S(2)}) collective-permute-start(f32[8,4096]{1,0:T(8,128)S(1)} %bitcast.84), channel_id=1, source_target_pairs={{0,32},{32,64},{64,0},{1,33},{33,65},{65,1},{2,34},{34,66},{66,2},... | collective-permute-start | bytes 393224 | tf_op jit(solution)/shard_map/ppermute | solution.py:86
  48.2 1.3 %collective-permute-done = f32[8,4096]{1,0:T(8,128)S(1)} collective-permute-done((f32[8,4096]{1,0:T(8,128)S(1)}, f32[8,4096]{1,0:T(8,128)S(1)}, u32[]{:S(2)}, u32[]{:S(2)}) %collective-permute-start) | collective-permute-done | bytes 131104 | tf_op jit(solution)/shard_map/ppermute | solution.py:86
  49.5 4.5 %collective-permute-done.1 = f32[8,4096]{1,0:T(8,128)S(1)} collective-permute-done((f32[8,4096]{1,0:T(8,128)S(1)}, f32[8,4096]{1,0:T(8,128)S(1)}, u32[]{:S(2)}, u32[]{:S(2)}) %collective-permute-start.1) | collective-permute-done | bytes 131104 | tf_op jit(solution)/shard_map/ppermute | solution.py:86
  54.1 2.6 %collective-permute-start.2 = (f32[8,4096]{1,0:T(8,128)S(1)}, f32[8,4096]{1,0:T(8,128)S(1)}, u32[]{:S(2)}, u32[]{:S(2)}) collective-permute-start(f32[8,4096]{1,0:T(8,128)S(1)} %select_add_fusion), channel_id=1, source_target_pairs={{0,384},{96,480},{192,576},{288,672},{384,0},{480,96},{576,192},{6... | collective-permute-start | bytes 393224 | tf_op jit(solution)/shard_map/ppermute | solution.py:100
  56.9 7.9 %collective-permute-done.2 = f32[8,4096]{1,0:T(8,128)S(1)} collective-permute-done((f32[8,4096]{1,0:T(8,128)S(1)}, f32[8,4096]{1,0:T(8,128)S(1)}, u32[]{:S(2)}, u32[]{:S(2)}) %collective-permute-start.2) | collective-permute-done | bytes 131104 | tf_op jit(solution)/shard_map/ppermute | solution.py:100
  64.8 4.9 %collective-permute-start.3 = (f32[8,4096]{1,0:T(8,128)S(1)}, f32[8,4096]{1,0:T(8,128)S(1)}, u32[]{:S(2)}, u32[]{:S(2)}) collective-permute-start(f32[8,4096]{1,0:T(8,128)S(1)} %add.182), channel_id=1, source_target_pairs={{0,192},{96,288},{192,0},{288,96},{384,576},{480,672},{576,384},{6... | collective-permute-start | bytes 393224 | tf_op jit(solution)/shard_map/ppermute | solution.py:100
  69.7 1.0 fusion.6
  70.7 1.5 %collective-permute-done.3 = f32[8,4096]{1,0:T(8,128)S(1)} collective-permute-done((f32[8,4096]{1,0:T(8,128)S(1)}, f32[8,4096]{1,0:T(8,128)S(1)}, u32[]{:S(2)}, u32[]{:S(2)}) %collective-permute-start.3) | collective-permute-done | bytes 131104 | tf_op jit(solution)/shard_map/ppermute | solution.py:100
  72.2 3.1 %collective-permute-start.4 = (f32[8,4096]{1,0:T(8,128)S(1)}, f32[8,4096]{1,0:T(8,128)S(1)}, u32[]{:S(2)}, u32[]{:S(2)}) collective-permute-start(f32[8,4096]{1,0:T(8,128)S(1)} %add.183), channel_id=1, source_target_pairs={{0,96},{96,0},{192,288},{288,192},{384,480},{480,384},{576,672},{6... | collective-permute-start | bytes 393224 | tf_op jit(solution)/shard_map/ppermute | solution.py:100
  75.5 0.7 fusion
  76.2 0.9 copy.21
  77.0 10.7 %all-to-all-start.1 = ((f32[2,32,8,128]{3,2,0,1:T(8,128)}), f32[2,32,8,128]{3,2,0,1:T(8,128)S(1)}, u32[]{:S(2)}, u32[]{:S(2)}) async-start(f32[2,32,8,128]{3,2,0,1:T(8,128)} %copy.21), calls=%async_computation.1 | async-start | bytes 524288 | tf_op jit(solution)/shard_map/all_to_all | solution.py:132
  87.8 0.7 add_multiply_fusion
  88.5 14.9 %all-to-all-done.1 = f32[2,32,8,128]{3,2,0,1:T(8,128)S(1)} async-done(((f32[2,32,8,128]{3,2,0,1:T(8,128)}), f32[2,32,8,128]{3,2,0,1:T(8,128)S(1)}, u32[]{:S(2)}, u32[]{:S(2)}) %all-to-all-start.1) | async-done | bytes 262176 | tf_op jit(solution)/shard_map/all_to_all | solution.py:132
  103.3 0.8 fusion.33
  (34 shorter events, 3.6 us)
Async XLA Ops:
  0.6 21.3 %copy-start = (f32[8,4096]{1,0:T(8,128)S(1)}, f32[8,4096]{1,0:T(8,128)}, u32[]{:S(2)}) copy-start(f32[8,4096]{1,0:T(8,128)} %param.9) | copy-start | bytes 393220
  2.5 31.9 %all-to-all-start = ((f32[2,32,8,128]{3,2,0,1:T(8,128)}), f32[2,32,8,128]{3,2,0,1:T(8,128)S(1)}, u32[]{:S(2)}, u32[]{:S(2)}) async-start(f32[2,32,8,128]{3,2,0,1:T(8,128)} %copy.19), calls=%async_computation | async-start | bytes 524288 | tf_op jit(solution)/shard_map/all_to_all | solution.py:127
  38.1 11.4 %collective-permute-start = (f32[8,4096]{1,0:T(8,128)S(1)}, f32[8,4096]{1,0:T(8,128)S(1)}, u32[]{:S(2)}, u32[]{:S(2)}) collective-permute-start(f32[8,4096]{1,0:T(8,128)S(1)} %bitcast.83), channel_id=1, source_target_pairs={{0,64},{32,0},{64,32},{1,65},{33,1},{65,33},{2,66},{34,2},{66,34},... | collective-permute-start | bytes 393224 | tf_op jit(solution)/shard_map/ppermute | solution.py:86
  46.2 7.8 %collective-permute-start.1 = (f32[8,4096]{1,0:T(8,128)S(1)}, f32[8,4096]{1,0:T(8,128)S(1)}, u32[]{:S(2)}, u32[]{:S(2)}) collective-permute-start(f32[8,4096]{1,0:T(8,128)S(1)} %bitcast.84), channel_id=1, source_target_pairs={{0,32},{32,64},{64,0},{1,33},{33,65},{65,1},{2,34},{34,66},{66,2},... | collective-permute-start | bytes 393224 | tf_op jit(solution)/shard_map/ppermute | solution.py:86
  54.1 10.6 %collective-permute-start.2 = (f32[8,4096]{1,0:T(8,128)S(1)}, f32[8,4096]{1,0:T(8,128)S(1)}, u32[]{:S(2)}, u32[]{:S(2)}) collective-permute-start(f32[8,4096]{1,0:T(8,128)S(1)} %select_add_fusion), channel_id=1, source_target_pairs={{0,384},{96,480},{192,576},{288,672},{384,0},{480,96},{576,192},{6... | collective-permute-start | bytes 393224 | tf_op jit(solution)/shard_map/ppermute | solution.py:100
  64.8 7.4 %collective-permute-start.3 = (f32[8,4096]{1,0:T(8,128)S(1)}, f32[8,4096]{1,0:T(8,128)S(1)}, u32[]{:S(2)}, u32[]{:S(2)}) collective-permute-start(f32[8,4096]{1,0:T(8,128)S(1)} %add.182), channel_id=1, source_target_pairs={{0,192},{96,288},{192,0},{288,96},{384,576},{480,672},{576,384},{6... | collective-permute-start | bytes 393224 | tf_op jit(solution)/shard_map/ppermute | solution.py:100
  72.2 15.6 %collective-permute-start.4 = (f32[8,4096]{1,0:T(8,128)S(1)}, f32[8,4096]{1,0:T(8,128)S(1)}, u32[]{:S(2)}, u32[]{:S(2)}) collective-permute-start(f32[8,4096]{1,0:T(8,128)S(1)} %add.183), channel_id=1, source_target_pairs={{0,96},{96,0},{192,288},{288,192},{384,480},{480,384},{576,672},{6... | collective-permute-start | bytes 393224 | tf_op jit(solution)/shard_map/ppermute | solution.py:100
  77.0 26.3 %copy-start.4 = (f32[1,256,128]{2,1,0:T(8,128)S(1)}, f32[1,256,128]{2,1,0:T(8,128)}, u32[]{:S(2)}) copy-start(f32[1,256,128]{2,1,0:T(8,128)} %param.7) | copy-start | bytes 393220
  77.0 26.3 %all-to-all-start.1 = ((f32[2,32,8,128]{3,2,0,1:T(8,128)}), f32[2,32,8,128]{3,2,0,1:T(8,128)S(1)}, u32[]{:S(2)}, u32[]{:S(2)}) async-start(f32[2,32,8,128]{3,2,0,1:T(8,128)} %copy.21), calls=%async_computation.1 | async-start | bytes 524288 | tf_op jit(solution)/shard_map/all_to_all | solution.py:132
  87.7 15.6 %copy-start.1 = (f32[1,256,128]{2,1,0:T(8,128)S(1)}, f32[1,256,128]{2,1,0:T(8,128)}, u32[]{:S(2)}) copy-start(f32[1,256,128]{2,1,0:T(8,128)} %param.6) | copy-start | bytes 393220
  87.7 15.6 %copy-start.2 = (f32[1,256,128]{2,1,0:T(8,128)S(1)}, f32[1,256,128]{2,1,0:T(8,128)}, u32[]{:S(2)}) copy-start(f32[1,256,128]{2,1,0:T(8,128)} %param.8) | copy-start | bytes 393220
  87.8 15.6 %copy-start.3 = (f32[1,256,128]{2,1,0:T(8,128)S(1)}, f32[1,256,128]{2,1,0:T(8,128)}, u32[]{:S(2)}) copy-start(f32[1,256,128]{2,1,0:T(8,128)} %param.5) | copy-start | bytes 393220
